TPU v7x, 256 devices: a whole 4x4x8 slice. The times are simulated.
256 devices in a mesh: sample: 8 (over z_lo, x), lat: 32 (over z_hi, y, core).
Axes of the slice: x: 4, y: 4, z: 8 (z_hi: 4, z_lo: 2; z = z_hi * 2 + z_lo), core: 2. Of those that a mesh axis runs over, the one named last changes fastest.
Arguments:
- tokens: bfloat16 [8, 96, 180, 768], P('sample', 'lat'), may hold values from -6 to 6
- norm_gain: float32 [768], replicated, may hold values from 0.5 to 1.5
- norm_shift: float32 [768], replicated, may hold values from -0.5 to 0.5
- weight_one: float32 [2, 8, 96, 96], replicated, may hold values from -0.4375 to 0.4375
- bias_one: float32 [2, 8, 96], replicated, may hold values from -3 to 3
- weight_two: float32 [2, 8, 96, 96], replicated, may hold values from -0.4375 to 0.4375
- bias_two: float32 [2, 8, 96], replicated, may hold values from -0.12 to 0.12
- cotangent: bfloat16 [8, 96, 180, 768], P('sample', 'lat'), may hold values from -6 to 6
Outputs:
- block_out: bfloat16 [8, 96, 180, 768], P('sample', 'lat')
- grad_input: bfloat16 [8, 96, 180, 768], P('sample', 'lat')
- grad_gain: float32 [768], replicated
- grad_shift: float32 [768], replicated
- grad_weight_one: float32 [2, 8, 96, 96], replicated
- grad_bias_one: float32 [2, 8, 96], replicated
- grad_weight_two: float32 [2, 8, 96, 96], replicated
- grad_bias_two: float32 [2, 8, 96], replicated
All inputs are finite; a program needn't handle non-finite values.
Results may differ from a plain program's by a relative error of at most 0.001.
Values sent between devices are 32-bit elements; how exact they have to be, the bound alone decides.
No kernel may reach another device: no remote copies, remote signals or barrier semaphores. Data moves between devices by JAX's collectives and lax.ppermute only.
A program may use at most 128 MiB of HBM per device.

v0:
```python
import jax
import jax.numpy as jnp
from jax import lax
from jax.sharding import PartitionSpec as P

HIGHEST = lax.Precision.HIGHEST
SHRINK = 0.01
EPSILON = 1e-05


def lon_basis(cell_count, mode_count):
    cell_index = jnp.arange(cell_count, dtype=jnp.int32)[:, None]
    mode_index = jnp.arange(mode_count, dtype=jnp.int32)[None, :]
    phase_int = (cell_index * mode_index % cell_count).astype(jnp.float32)
    phase_angle = phase_int * (2.0 * jnp.pi / cell_count)
    keep_scale = (mode_index < cell_count // 2 + 1).astype(jnp.float32) / jnp.sqrt(
        jnp.float32(cell_count)
    )
    return jnp.stack(
        [jnp.cos(phase_angle) * keep_scale, -jnp.sin(phase_angle) * keep_scale], axis=1
    )


def lon_weight(cell_count, mode_count):
    mode_index = jnp.arange(mode_count, dtype=jnp.int32)
    single = jnp.logical_or(mode_index == 0, 2 * mode_index == cell_count)
    return jnp.where(single, 1.0, 2.0).astype(jnp.float32)


def lat_basis(row_count):
    row_index = jnp.arange(row_count, dtype=jnp.int32)
    phase_int = (row_index[:, None] * row_index[None, :] % row_count).astype(jnp.float32)
    phase_angle = phase_int * (2.0 * jnp.pi / row_count)
    norm_factor = 1.0 / jnp.sqrt(jnp.float32(row_count))
    return (jnp.cos(phase_angle) * norm_factor, jnp.sin(phase_angle) * norm_factor)


def lat_apply(values_in, cosine, sine_table, orient):
    cosine_part = jnp.einsum("ph,shrkc->sprkc", cosine, values_in, precision=HIGHEST)
    sine_part = jnp.einsum("ph,shrkc->sprkc", sine_table, values_in, precision=HIGHEST)
    real_part = cosine_part[:, :, 0] + orient * sine_part[:, :, 1]
    imag_part = cosine_part[:, :, 1] - orient * sine_part[:, :, 0]
    return jnp.stack([real_part, imag_part], axis=2)


def block_product(values_in, weights):

    def product_part(part_in, slot_index):
        return jnp.einsum("shkgi,gio->shkgo", part_in, weights[slot_index], precision=HIGHEST)

    real_input = values_in[:, :, 0]
    imag_input = values_in[:, :, 1]
    real_out = product_part(real_input, 0) - product_part(imag_input, 1)
    imag_out = product_part(imag_input, 0) + product_part(real_input, 1)
    return jnp.stack([real_out, imag_out], axis=2)


def block_adjoint(values_in, weights):

    def product_part(part_in, slot_index):
        return jnp.einsum("shkgo,gio->shkgi", part_in, weights[slot_index], precision=HIGHEST)

    real_input = values_in[:, :, 0]
    imag_input = values_in[:, :, 1]
    real_out = product_part(real_input, 0) + product_part(imag_input, 1)
    imag_out = product_part(imag_input, 0) - product_part(real_input, 1)
    return jnp.stack([real_out, imag_out], axis=2)


def weight_grad(inputs, upstream):

    def contract(left_side, right_side):
        return jnp.einsum("shkgi,shkgo->gio", left_side, right_side, precision=HIGHEST)

    real_input = inputs[:, :, 0]
    imag_input = inputs[:, :, 1]
    real_upper = upstream[:, :, 0]
    imag_upper = upstream[:, :, 1]
    first = contract(real_input, real_upper) + contract(imag_input, imag_upper)
    second = contract(real_input, imag_upper) - contract(imag_input, real_upper)
    return jnp.stack([first, second], axis=0)


def shrink(values):
    return values - SHRINK * values * lax.rsqrt(values * values + SHRINK * SHRINK)


def local(tokens, norm_gain, norm_shift, weight_one, bias_one, weight_two, bias_two, cotangent):
    lat_parts = lax.axis_size("lat")
    samples, local_rows, lon_cells, features = tokens.shape
    groups = weight_one.shape[1]
    block_size = weight_one.shape[2]
    lat_rows = local_rows * lat_parts
    kept_modes = lon_cells // 2 + 1
    padded = (kept_modes + lat_parts - 1) // lat_parts * lat_parts
    lon_table = lon_basis(lon_cells, padded)
    weighted = lon_table * lon_weight(lon_cells, padded)[None, None, :]
    cosine, sine_table = lat_basis(lat_rows)
    float_tokens = tokens.astype(jnp.float32)
    average = jnp.mean(float_tokens, axis=-1, keepdims=True)
    centred = float_tokens - average
    variance = jnp.mean(centred * centred, axis=-1, keepdims=True)
    inverse_std = lax.rsqrt(variance + EPSILON)
    normalized = centred * inverse_std
    normed = normalized * norm_gain + norm_shift
    upstream_out = cotangent.astype(jnp.float32)
    lon_spectrum = jnp.einsum("shwc,wrk->shrkc", normed, lon_table, precision=HIGHEST)
    cotangent_lon = jnp.einsum("shwc,wrk->shrkc", upstream_out, weighted, precision=HIGHEST)
    mode_shape = (samples, lat_rows, 2, padded // lat_parts, groups, block_size)
    gathered = lax.all_to_all(lon_spectrum, "lat", split_axis=3, concat_axis=1, tiled=True)
    spectrum = lat_apply(gathered, cosine, sine_table, 1.0).reshape(mode_shape)
    pre_inner = block_product(spectrum, weight_one) + bias_one[None, None, :, None]
    inner_act, gelu_back = jax.vjp(jax.nn.gelu, pre_inner)
    pre_outer = block_product(inner_act, weight_two) + bias_two[None, None, :, None]
    shrunk, shrink_back = jax.vjp(shrink, pre_outer)
    leaving = lat_apply(shrunk.reshape(gathered.shape), cosine, sine_table, -1.0)
    leaving, saved_state = (leaving, (spectrum, inner_act, gelu_back, shrink_back))
    returned = lax.all_to_all(leaving, "lat", split_axis=1, concat_axis=3, tiled=True)
    cotangent_modes = lax.all_to_all(cotangent_lon, "lat", split_axis=3, concat_axis=1, tiled=True)
    spectrum, inner_act, gelu_back, shrink_back = saved_state
    shrunk_grad = lat_apply(cotangent_modes, cosine, sine_table, 1.0).reshape(mode_shape)
    outer_grad = shrink_back(shrunk_grad)[0]
    weight_two_grad = weight_grad(inner_act, outer_grad)
    bias_two_grad = jnp.sum(outer_grad, axis=(0, 1, 3))
    inner_grad = gelu_back(block_adjoint(outer_grad, weight_two))[0]
    weight_one_grad = weight_grad(spectrum, inner_grad)
    bias_one_grad = jnp.sum(inner_grad, axis=(0, 1, 3))
    spectrum_grad = block_adjoint(inner_grad, weight_one).reshape(cotangent_modes.shape)
    adjoint_modes = lat_apply(spectrum_grad, cosine, sine_table, -1.0)
    adjoint_modes, spectral_grads = (
        adjoint_modes,
        (weight_one_grad, bias_one_grad, weight_two_grad, bias_two_grad),
    )
    adjoint_rows = lax.all_to_all(adjoint_modes, "lat", split_axis=1, concat_axis=3, tiled=True)
    filtered = jnp.einsum("shrkc,wrk->shwc", returned, weighted, precision=HIGHEST)
    block_out = (float_tokens + normed + filtered).astype(jnp.bfloat16)
    normed_grad = upstream_out + jnp.einsum(
        "shrkc,wrk->shwc", adjoint_rows, lon_table, precision=HIGHEST
    )
    hat_grad = normed_grad * norm_gain
    hat_mean = jnp.mean(hat_grad, axis=-1, keepdims=True)
    cross_mean = jnp.mean(hat_grad * normalized, axis=-1, keepdims=True)
    grad_input = upstream_out + inverse_std * (hat_grad - hat_mean - normalized * cross_mean)
    local_gain = jnp.sum(normed_grad * normalized, axis=(0, 1, 2))
    local_shift = jnp.sum(normed_grad, axis=(0, 1, 2))
    summed = lax.psum(
        (
            spectral_grads[0],
            spectral_grads[1],
            spectral_grads[2],
            spectral_grads[3],
            local_gain,
            local_shift,
        ),
        ("sample", "lat"),
    )
    return (
        block_out,
        grad_input.astype(jnp.bfloat16),
        summed[4],
        summed[5],
        summed[0],
        summed[1],
        summed[2],
        summed[3],
    )


def solution(mesh):
    placed = (
        P("sample", "lat", None, None),
        P(),
        P(),
        P(),
        P(),
        P(),
        P(),
        P("sample", "lat", None, None),
    )
    return jax.shard_map(
        local,
        mesh=mesh,
        in_specs=placed,
        out_specs=(
            P("sample", "lat", None, None),
            P("sample", "lat", None, None),
            P(),
            P(),
            P(),
            P(),
            P(),
            P(),
        ),
        check_vma=False,
    )
```

profile of v0, /device:TPU:1, one launch (start us, length us, event | category | flops | bytes accessed | tf_op | source)
XLA Modules:
  0.0 549.6 jit_solution(13453059925194760207)
XLA Ops:
  7.2 1.4 convert_reduce_fusion
  8.6 1.6 fusion.29
  10.7 1.9 fusion.53
  12.6 2.6 copy.100
  15.2 12.9 %all-to-all-start = ((f32[1,3,2,96,768]{4,2,1,0,3:T(2,128)}), f32[1,3,2,96,768]{4,2,1,0,3:T(2,128)S(1)}, u32[]{:S(2)}, u32[]{:S(2)}) async-start(f32[1,3,2,96,768]{4,2,1,0,3:T(2,128)} %copy.100), calls=%async_computation | async-start | bytes 3538944 | tf_op jit(solution)/shard_map/all_to_all | solution.py:110
  29.1 2.6 copy.114
  31.7 39.2 %all-to-all-done = f32[1,3,2,96,768]{4,2,1,0,3:T(2,128)S(1)} async-done(((f32[1,3,2,96,768]{4,2,1,0,3:T(2,128)}), f32[1,3,2,96,768]{4,2,1,0,3:T(2,128)S(1)}, u32[]{:S(2)}, u32[]{:S(2)}) %all-to-all-start) | async-done | bytes 1769504 | tf_op jit(solution)/shard_map/all_to_all | solution.py:110
  70.9 6.8 %all-to-all-start.2 = ((f32[1,3,2,96,768]{4,2,1,0,3:T(2,128)}), f32[1,3,2,96,768]{4,2,1,0,3:T(2,128)S(1)}, u32[]{:S(2)}, u32[]{:S(2)}) async-start(f32[1,3,2,96,768]{4,2,1,0,3:T(2,128)} %copy.114), calls=%async_computation.2 | async-start | bytes 3538944 | tf_op jit(solution)/shard_map/all_to_all | solution.py:119
  78.9 1.9 fusion.44
  80.8 3.2 fusion.41
  84.0 37.5 %all-to-all-done.2 = f32[1,3,2,96,768]{4,2,1,0,3:T(2,128)S(1)} async-done(((f32[1,3,2,96,768]{4,2,1,0,3:T(2,128)}), f32[1,3,2,96,768]{4,2,1,0,3:T(2,128)S(1)}, u32[]{:S(2)}, u32[]{:S(2)}) %all-to-all-start.2) | async-done | bytes 1769504 | tf_op jit(solution)/shard_map/all_to_all | solution.py:119
  122.7 3.1 fusion.50
  125.9 3.1 fusion.47
  129.0 1.3 slice_add_fusion.1
  131.2 2.8 reshape.766
  134.0 1.8 copy.127
  135.9 2.0 fusion.105
  137.9 2.0 fusion.103
  140.0 2.0 fusion.60
  142.0 2.0 fusion.61
  145.6 2.2 fusion.75
  147.8 2.2 fusion.74
  150.1 1.5 slice_subtract_fusion
  151.6 3.2 stack.96
  154.7 2.7 stack.95
  157.5 1.6 copy_dynamic-update-slice_fusion.1
  163.0 2.1 fusion.225
  170.4 2.6 fusion.227
  174.2 2.2 fusion.78
  177.6 1.8 copy.122
  179.4 2.6 stack.105
  182.0 3.0 fusion.64
  185.0 1.7 copy.121
  186.7 2.7 stack.104
  189.4 3.4 convolution_bitcast_fusion
  192.9 1.9 convolution_bitcast_fusion.1
  195.1 2.8 copy.123
  197.9 6.4 %all-to-all-start.3 = ((f32[1,96,2,3,768]{4,2,3,0,1:T(2,128)}), f32[1,96,2,3,768]{4,2,3,0,1:T(2,128)}, u32[]{:S(2)}, u32[]{:S(2)}) async-start(f32[1,96,2,3,768]{4,2,3,0,1:T(2,128)} %copy.123), calls=%async_computation.3 | async-start | bytes 3538944 | tf_op jit(solution)/shard_map/all_to_all | solution.py:134
  205.0 3.0 copy.110
  208.0 2.6 stack.92
  210.6 3.1 copy.109
  213.6 2.6 stack.91
  216.2 3.9 convolution_bitcast_fusion.2
  220.2 2.3 convolution_bitcast_fusion.3
  222.8 2.6 copy.111
  225.5 22.7 %all-to-all-done.3 = f32[1,96,2,3,768]{4,2,3,0,1:T(2,128)} async-done(((f32[1,96,2,3,768]{4,2,3,0,1:T(2,128)}), f32[1,96,2,3,768]{4,2,3,0,1:T(2,128)}, u32[]{:S(2)}, u32[]{:S(2)}) %all-to-all-start.3) | async-done | bytes 1769504 | tf_op jit(solution)/shard_map/all_to_all | solution.py:134
  248.2 5.9 %all-to-all-start.1 = ((f32[1,96,2,3,768]{4,2,3,0,1:T(2,128)}), f32[1,96,2,3,768]{4,2,3,0,1:T(2,128)}, u32[]{:S(2)}, u32[]{:S(2)}) async-start(f32[1,96,2,3,768]{4,2,3,0,1:T(2,128)} %copy.111), calls=%async_computation.1 | async-start | bytes 3538944 | tf_op jit(solution)/shard_map/all_to_all | solution.py:118
  254.5 3.9 convolution_bitcast_fusion.7
  258.5 2.5 convolution_bitcast_fusion.5
  261.0 3.0 convolution_bitcast_fusion.11
  264.1 1.7 convolution_bitcast_fusion.9
  265.7 2.5 fusion.71
  268.3 2.7 fusion.73
  271.0 1.7 fusion.69
  272.7 1.7 fusion.67
  275.7 2.2 copy.124
  277.9 2.4 fusion.28
  280.3 15.8 %all-to-all-done.1 = f32[1,96,2,3,768]{4,2,3,0,1:T(2,128)} async-done(((f32[1,96,2,3,768]{4,2,3,0,1:T(2,128)}), f32[1,96,2,3,768]{4,2,3,0,1:T(2,128)}, u32[]{:S(2)}, u32[]{:S(2)}) %all-to-all-start.1) | async-done | bytes 1769504 | tf_op jit(solution)/shard_map/all_to_all | solution.py:118
  296.0 2.1 copy.112
  298.2 2.8 fusion.32
  301.0 77.0 %all-reduce = (f32[768]{0:T(1024)}, f32[768]{0:T(1024)}, f32[2,8,96]{2,1,0:T(8,128)}, f32[2,8,96]{2,1,0:T(8,128)}) all-reduce(f32[768]{0:T(1024)S(1)} %get-tuple-element.8, f32[768]{0:T(1024)S(1)} %get-tuple-element.11, f32[2,8,96]{2,1,0:T(8,128)S(1)} %copy-done.38, ...), channel_id=1, replica_groups=mesh['sample'=8,'lat'=32] {'sample','lat'}, use_global_device_ids=true, to_apply=%region_5.6 | all-reduce | flops 4608 | bytes 36864 | tf_op jit(solution)/shard_map/psum | solution.py:146
  378.0 1.6 fusion.30
  379.6 159.9 %all-reduce.4.cloned.1.call-done = (f32[2,8,96,96]{3,2,1,0:T(8,128)}, f32[2,8,96,96]{3,2,1,0:T(8,128)}) async-done(((f32[2,8,96,96]{3,2,1,0:T(8,128)}, f32[2,8,96,96]{3,2,1,0:T(8,128)}), (f32[2,8,96,96]{3,2,1,0:T(8,128)}, f32[2,8,96,96]{3,2,1,0:T(8,128)})) %all-reduce.4.cloned.1.call-update) | async-done | bytes 1179664 | tf_op jit(solution)/shard_map/psum | solution.py:146
  539.6 2.1 copy.187
  (128 shorter events, 21.9 us)
Async XLA Ops:
  7.2 3.5 copy-start.6
  7.2 3.5 copy-start.41
  7.2 3.5 copy-start.44
  10.6 17.4 %copy-start.30 = (f32[180,1,96]{2,0,1:T(8,128)}, f32[180,1,96]{2,0,1:T(8,128)S(1)}, u32[]{:S(2)}) copy-start(f32[180,1,96]{2,0,1:T(8,128)S(1)} %get-tuple-element.30) | copy-start | bytes 207364
  10.7 17.4 %copy-start.32 = (f32[180,1,96]{2,0,1:T(8,128)}, f32[180,1,96]{2,0,1:T(8,128)S(1)}, u32[]{:S(2)}) copy-start(f32[180,1,96]{2,0,1:T(8,128)S(1)} %get-tuple-element.31) | copy-start | bytes 207364
  15.2 12.9 %copy-start.26 = (bf16[1,3,180,768]{3,2,1,0:T(8,128)(2,1)S(1)}, bf16[1,3,180,768]{3,2,1,0:T(8,128)(2,1)}, u32[]{:S(2)}) copy-start(bf16[1,3,180,768]{3,2,1,0:T(8,128)(2,1)} %param.15) | copy-start | bytes 2488324
  15.2 55.7 %all-to-all-start = ((f32[1,3,2,96,768]{4,2,1,0,3:T(2,128)}), f32[1,3,2,96,768]{4,2,1,0,3:T(2,128)S(1)}, u32[]{:S(2)}, u32[]{:S(2)}) async-start(f32[1,3,2,96,768]{4,2,1,0,3:T(2,128)} %copy.100), calls=%async_computation | async-start | bytes 3538944 | tf_op jit(solution)/shard_map/all_to_all | solution.py:110
  28.1 3.5 copy-start.46
  70.9 50.7 %all-to-all-start.2 = ((f32[1,3,2,96,768]{4,2,1,0,3:T(2,128)}), f32[1,3,2,96,768]{4,2,1,0,3:T(2,128)S(1)}, u32[]{:S(2)}, u32[]{:S(2)}) async-start(f32[1,3,2,96,768]{4,2,1,0,3:T(2,128)} %copy.114), calls=%async_computation.2 | async-start | bytes 3538944 | tf_op jit(solution)/shard_map/all_to_all | solution.py:119
  125.9 3.1 copy-start.22
  131.2 4.7 copy-start.10
  135.9 4.0 copy-start.4
  142.0 2.1 copy-start.14
  142.0 2.1 copy-start.36
  144.1 1.1 copy-start.16
  144.1 1.6 copy-start.8
  145.6 15.0 %copy-start.2 = (f32[1,96,2,3,8,96]{5,1,3,4,2,0:T(8,128)}, f32[1,96,2,3,8,96]{5,1,3,4,2,0:T(8,128)S(1)}, u32[]{:S(2)}) copy-start(f32[1,96,2,3,8,96]{5,1,3,4,2,0:T(8,128)S(1)} %multiply_multiply_fusion.2) | copy-start | bytes 5308420
  145.6 4.5 copy-start.21
  147.8 2.3 copy-start.20
  157.5 1.6 copy-start.9
  157.5 1.9 copy-start.25
  159.3 1.3 copy-start.24
  160.6 1.9 copy-start.13
  160.6 1.7 copy-start.23
  162.3 2.8 copy-start.12
  162.3 0.7 copy-start.39
  168.8 1.3 copy-start.15
  168.8 1.6 copy-start.17
  170.4 2.6 copy-start.11
  173.0 3.4 copy-start
  189.4 3.5 copy-start.18
  189.4 3.5 copy-start.19
  197.9 6.4 %copy-start.40 = (f32[2,8,96]{2,1,0:T(8,128)S(1)}, f32[2,8,96]{2,1,0:T(8,128)}, u32[]{:S(2)}) copy-start(f32[2,8,96]{2,1,0:T(8,128)} %param.14) | copy-start | bytes 18436
  197.9 50.2 %all-to-all-start.3 = ((f32[1,96,2,3,768]{4,2,3,0,1:T(2,128)}), f32[1,96,2,3,768]{4,2,3,0,1:T(2,128)}, u32[]{:S(2)}, u32[]{:S(2)}) async-start(f32[1,96,2,3,768]{4,2,3,0,1:T(2,128)} %copy.123), calls=%async_computation.3 | async-start | bytes 3538944 | tf_op jit(solution)/shard_map/all_to_all | solution.py:134
  210.6 5.7 %copy-start.43 = (f32[2,768]{1,0:T(2,128)S(1)}, f32[2,768]{1,0:T(2,128)}, u32[]{:S(2)}) copy-start(f32[2,768]{1,0:T(2,128)} %add.279) | copy-start | bytes 18436
  216.2 3.9 copy-start.28
  216.2 3.9 copy-start.29
  248.2 47.9 %all-to-all-start.1 = ((f32[1,96,2,3,768]{4,2,3,0,1:T(2,128)}), f32[1,96,2,3,768]{4,2,3,0,1:T(2,128)}, u32[]{:S(2)}, u32[]{:S(2)}) async-start(f32[1,96,2,3,768]{4,2,3,0,1:T(2,128)} %copy.111), calls=%async_computation.1 | async-start | bytes 3538944 | tf_op jit(solution)/shard_map/all_to_all | solution.py:118
  254.1 285.5 %all-reduce.4.cloned.1.call-start = ((), (), s32[]{:S(2)}) async-start(), calls=%async_computation.4 | async-start | bytes 3145728 | tf_op jit(solution)/shard_map/psum | solution.py:146
  254.5 3.9 copy-start.3
  258.4 2.5 copy-start.1
  261.0 3.1 copy-start.5
  275.6 2.3 copy-start.7
  275.6 2.3 copy-start.27
  275.6 2.3 copy-start.31
  275.6 2.3 copy-start.33
  275.7 2.3 copy-start.42
  296.0 2.1 copy-start.34
  296.0 2.1 copy-start.45
  296.0 2.2 copy-start.47
  298.2 2.8 copy-start.37
  298.2 2.8 copy-start.38
  539.6 2.1 copy-start.35
Sparse Core Ops, SparseCore 0:
  275.7 263.7 all-reduce.3
where the time goes:
time: 557 us; the launch traced here: 550 us
  waiting for transfers between devices  275 us (49%)
  matrix products  77.9 us (14%)
  blocking collectives  77 us (14%)
  local copies, waits for them, and re-layouts  56.8 us (10%)
  starting transfers between devices  32.4 us (6%)
  other arithmetic  15.3 us (3%)
  between operations  15.1 us (3%)
    psum x1, waiting for transfers between devices, local(): lax.psum((spectral_grads[0], spectral_grads[1], spectral_grads[2], spectr...  160 us
    psum x1, blocking collectives, local(): lax.psum((spectral_grads[0], spectral_grads[1], spectral_grads[2], spectr...  77 us
    all_to_all x1, waiting for transfers between devices, local(): lax.all_to_all(lon_spectrum, 'lat', split_axis=3, concat_axis=1, tiled=True)  39.2 us
    all_to_all x1, waiting for transfers between devices, local(): lax.all_to_all(cotangent_lon, 'lat', split_axis=3, concat_axis=1, tiled=T...  37.5 us
    all_to_all x1, waiting for transfers between devices, local(): lax.all_to_all(adjoint_modes, 'lat', split_axis=1, concat_axis=3, tiled=T...  22.7 us
    dot_general x8, matrix products, contract(): jnp.einsum('shkgi,shkgo->gio', left_side, right_side, precision=HIGHEST)  19.7 us
    all_to_all x1, waiting for transfers between devices, local(): lax.all_to_all(leaving, 'lat', split_axis=1, concat_axis=3, tiled=True)  15.8 us
    dot_general x8, matrix products, product_part(): jnp.einsum('shkgi,gio->shkgo', part_in, weights[slot_index], precision=HI...  15 us
  transfers between devices with their start and end apart: 5, of which 5 were waited for; matrix products, arithmetic and copies ran while one was open for 11% of the time, Pallas kernels for 0%

commit v1 on v0

--- a/solution.py
+++ b/solution.py
@@ -83,6 +83,25 @@
 
 def shrink(values):
     return values - SHRINK * values * lax.rsqrt(values * values + SHRINK * SHRINK)
+
+
+def flat_sum(parts, axes):
+    count = 1
+    for name in axes:
+        count *= lax.axis_size(name)
+    flat = jnp.concatenate([part.reshape(-1) for part in parts])
+    size = flat.shape[0]
+    chunk = -(-size // (count * 128)) * 128
+    flat = jnp.pad(flat, (0, count * chunk - size)).reshape(count, chunk)
+    reduced = lax.all_to_all(flat, axes, 0, 0, tiled=True).sum(axis=0)
+    spread = jnp.broadcast_to(reduced[None], (count, chunk))
+    whole = lax.all_to_all(spread, axes, 0, 0, tiled=True).reshape(-1)
+    results = []
+    offset = 0
+    for part in parts:
+        results.append(whole[offset : offset + part.size].reshape(part.shape))
+        offset += part.size
+    return tuple(results)
 
 
 def local(tokens, norm_gain, norm_shift, weight_one, bias_one, weight_two, bias_two, cotangent):
@@ -143,7 +162,7 @@
     grad_input = upstream_out + inverse_std * (hat_grad - hat_mean - normalized * cross_mean)
     local_gain = jnp.sum(normed_grad * normalized, axis=(0, 1, 2))
     local_shift = jnp.sum(normed_grad, axis=(0, 1, 2))
-    summed = lax.psum(
+    summed = flat_sum(
         (
             spectral_grads[0],
             spectral_grads[1],

time: 557 us -> 423 us (0.76)
  blocking collectives: 77 us -> 0 us
  waiting for transfers between devices: 275 us -> 198 us
  starting transfers between devices: 32.4 us -> 50.3 us
  between operations: 15.1 us -> 1.88 us
  matrix products: 77.9 us -> 85.5 us
    psum x1 -> x0, waiting for transfers between devices: 160 us -> none  [local(): lax.psum((spectral_grads[0], spectral_grads[1], spectral_grads[2], spectr...]
    psum x1 -> x0, blocking collectives: 77 us -> none  [local(): lax.psum((spectral_grads[0], spectral_grads[1], spectral_grads[2], spectr...]
    all_to_all x0 -> x2, waiting for transfers between devices: none -> 51.3 us  [the longest x1 30.8 us: flat_sum(): whole = lax.all_to_all(spread, axes, 0, 0, tiled=True).reshape(-1)]
    all_to_all x1, waiting for transfers between devices: 15.8 us -> 40.4 us  [local(): lax.all_to_all(leaving, 'lat', split_axis=1, concat_axis=3, tiled=True)]
    all_to_all x0 -> x2, starting transfers between devices: none -> 19.4 us  [the longest x1 9.74 us: flat_sum(): whole = lax.all_to_all(spread, axes, 0, 0, tiled=True).reshape(-1)]
    reshape x0 -> x8, local copies, waits for them, and re-layouts: none -> 7.78 us  [the longest x4 4.22 us: flat_sum(): flat = jnp.concatenate([part.reshape(-1) for part in parts])]
    all_to_all x1, waiting for transfers between devices: 22.7 us -> 29.5 us  [local(): lax.all_to_all(adjoint_modes, 'lat', split_axis=1, concat_axis=3, tiled=T...]
  transfers between devices with their start and end apart: 5 -> 6, of which waited for: 5 -> 6; matrix products, arithmetic and copies ran while one was open for 11% -> 11% of each run, Pallas kernels for 0% -> 0%
where the time goes in v1:
time: 423 us; the launch traced here: 415 us
  waiting for transfers between devices  198 us (47%)
  matrix products  85.5 us (20%)
  local copies, waits for them, and re-layouts  61.4 us (15%)
  starting transfers between devices  50.3 us (12%)
  other arithmetic  18.3 us (4%)
    all_to_all x1, waiting for transfers between devices, local(): lax.all_to_all(leaving, 'lat', split_axis=1, concat_axis=3, tiled=True)  40.4 us
    all_to_all x1, waiting for transfers between devices, local(): lax.all_to_all(lon_spectrum, 'lat', split_axis=3, concat_axis=1, tiled=True)  39.2 us
    all_to_all x1, waiting for transfers between devices, local(): lax.all_to_all(cotangent_lon, 'lat', split_axis=3, concat_axis=1, tiled=T...  37.5 us
    all_to_all x1, waiting for transfers between devices, flat_sum(): whole = lax.all_to_all(spread, axes, 0, 0, tiled=True).reshape(-1)  30.8 us
    all_to_all x1, waiting for transfers between devices, local(): lax.all_to_all(adjoint_modes, 'lat', split_axis=1, concat_axis=3, tiled=T...  29.5 us
    dot_general x8, matrix products, contract(): jnp.einsum('shkgi,shkgo->gio', left_side, right_side, precision=HIGHEST)  24.3 us
    all_to_all x1, waiting for transfers between devices, flat_sum(): reduced = lax.all_to_all(flat, axes, 0, 0, tiled=True).sum(axis=0)  20.5 us
    dot_general x8, matrix products, product_part(): jnp.einsum('shkgi,gio->shkgo', part_in, weights[slot_index], precision=HI...  14.9 us
  transfers between devices with their start and end apart: 6, of which 6 were waited for; matrix products, arithmetic and copies ran while one was open for 11% of the time, Pallas kernels for 0%

profile of v1, /device:TPU:1, one launch (start us, length us, event | category | flops | bytes accessed | tf_op | source)
XLA Modules:
  0.0 415.3 jit_solution(15573337222619394718)
XLA Ops:
  2.1 1.6 fusion.29
  4.2 1.9 fusion.53
  6.1 2.6 copy.168
  8.7 12.9 %all-to-all-start = ((f32[1,3,2,96,768]{4,2,1,0,3:T(2,128)}), f32[1,3,2,96,768]{4,2,1,0,3:T(2,128)S(1)}, u32[]{:S(2)}, u32[]{:S(2)}) async-start(f32[1,3,2,96,768]{4,2,1,0,3:T(2,128)} %copy.168), calls=%async_computation | async-start | bytes 3538944 | tf_op jit(solution)/shard_map/all_to_all | solution.py:129
  22.6 2.6 copy.182
  25.2 39.2 %all-to-all-done = f32[1,3,2,96,768]{4,2,1,0,3:T(2,128)S(1)} async-done(((f32[1,3,2,96,768]{4,2,1,0,3:T(2,128)}), f32[1,3,2,96,768]{4,2,1,0,3:T(2,128)S(1)}, u32[]{:S(2)}, u32[]{:S(2)}) %all-to-all-start) | async-done | bytes 1769504 | tf_op jit(solution)/shard_map/all_to_all | solution.py:129
  64.4 6.8 %all-to-all-start.2 = ((f32[1,3,2,96,768]{4,2,1,0,3:T(2,128)}), f32[1,3,2,96,768]{4,2,1,0,3:T(2,128)S(1)}, u32[]{:S(2)}, u32[]{:S(2)}) async-start(f32[1,3,2,96,768]{4,2,1,0,3:T(2,128)} %copy.182), calls=%async_computation.2 | async-start | bytes 3538944 | tf_op jit(solution)/shard_map/all_to_all | solution.py:138
  72.4 1.9 fusion.44
  74.3 3.1 fusion.41
  77.4 37.5 %all-to-all-done.2 = f32[1,3,2,96,768]{4,2,1,0,3:T(2,128)S(1)} async-done(((f32[1,3,2,96,768]{4,2,1,0,3:T(2,128)}), f32[1,3,2,96,768]{4,2,1,0,3:T(2,128)S(1)}, u32[]{:S(2)}, u32[]{:S(2)}) %all-to-all-start.2) | async-done | bytes 1769504 | tf_op jit(solution)/shard_map/all_to_all | solution.py:138
  116.2 3.1 fusion.50
  119.3 3.1 fusion.47
  124.6 2.8 reshape.804
  127.5 2.0 copy.195
  129.6 2.0 fusion.105
  131.6 2.0 fusion.103
  133.6 2.0 fusion.60
  135.7 2.0 fusion.61
  139.3 2.2 fusion.75
  141.5 2.2 fusion.74
  145.2 2.9 stack.96
  148.0 2.7 stack.95
  150.8 1.6 copy_dynamic-update-slice_fusion.1
  156.3 2.1 fusion.225
  158.4 3.2 convolution_bitcast_fusion.7
  161.7 3.2 convolution_bitcast_fusion.5
  166.1 1.6 fusion.76
  170.5 2.6 fusion.227
  174.3 2.2 fusion.78
  177.7 1.8 copy.190
  179.5 2.6 stack.105
  182.1 2.6 fusion.64
  184.7 1.7 copy.189
  186.4 2.6 stack.104
  189.0 4.7 %convolution_bitcast_fusion = f32[1,96,2,3,768]{4,1,3,2,0:T(8,128)} fusion(f32[1,96,1,3,768]{4,1,3,2,0:T(8,128)} %stack.105, f32[1,96,1,3,768]{4,1,3,2,0:T(8,128)} %stack.104), kind=kOutput, calls=%fused_computation.64 | convolution fusion | flops 510142464 | bytes 3538944 | tf_op jit(solution)/shard_map/ph,shrkc->sprkc/dot_general | solution.py:40
  193.7 3.1 convolution_bitcast_fusion.1
  197.5 5.2 %fusion.71 = f32[1,8,96,96]{3,2,1,0:T(8,128)} fusion(f32[8,96,96]{2,1,0:T(8,128)} %convolution_bitcast_fusion.7, f32[1,96,2,3,8,96]{5,1,3,4,2,0:T(8,128)} %copy-done.2, f32[1,96,2,3,8,96]{5,1,3,4,2,0:T(8,128)} %copy-done), kind=kOutput, calls=%fused_computation.97 | convolution fusion | flops 254877696 | bytes 3047424 | tf_op jit(solution)/shard_map/shkgi,shkgo->gio/dot_general | solution.py:73
  202.8 4.7 %fusion.73 = f32[1,8,96,96]{3,2,1,0:T(8,128)} fusion(f32[8,96,96]{2,1,0:T(8,128)} %convolution_bitcast_fusion.5, f32[1,96,2,3,8,96]{5,1,3,4,2,0:T(8,128)} %copy-done.2, f32[1,96,2,3,8,96]{5,1,3,4,2,0:T(8,128)S(1)} %copy-done.1), kind=kOutput, calls=%fused_computation.99 | convolution fusion | flops 254877696 | bytes 3047424 | tf_op jit(solution)/shard_map/shkgi,shkgo->gio/dot_general | solution.py:73
  207.9 2.6 copy.191
  210.4 6.1 %all-to-all-start.3 = ((f32[1,96,2,3,768]{4,2,3,0,1:T(2,128)}), f32[1,96,2,3,768]{4,2,3,0,1:T(2,128)}, u32[]{:S(2)}, u32[]{:S(2)}) async-start(f32[1,96,2,3,768]{4,2,3,0,1:T(2,128)} %copy.191), calls=%async_computation.3 | async-start | bytes 3538944 | tf_op jit(solution)/shard_map/all_to_all | solution.py:153
  216.5 2.1 pad_maximum_fusion.4
  218.6 2.4 reshape.818
  221.7 3.0 convolution_bitcast_fusion.11
  224.7 1.6 convolution_bitcast_fusion.9
  226.4 1.6 fusion.69
  228.0 1.6 fusion.67
  231.0 29.5 %all-to-all-done.3 = f32[1,96,2,3,768]{4,2,3,0,1:T(2,128)} async-done(((f32[1,96,2,3,768]{4,2,3,0,1:T(2,128)}), f32[1,96,2,3,768]{4,2,3,0,1:T(2,128)}, u32[]{:S(2)}, u32[]{:S(2)}) %all-to-all-start.3) | async-done | bytes 1769504 | tf_op jit(solution)/shard_map/all_to_all | solution.py:153
  260.5 2.2 copy.192
  262.8 3.3 fusion.28
  267.4 9.6 %all-to-all-start.4 = ((f32[256,1,1280]{2,1,0:T(1,128)}), f32[256,1,1280]{2,1,0:T(1,128)}, u32[]{:S(2)}, u32[]{:S(2)}) async-start(f32[256,1,1280]{2,1,0:T(1,128)} %bitcast.367), calls=%async_computation.4 | async-start | bytes 2621440 | tf_op jit(solution)/shard_map/all_to_all | solution.py:96
  277.1 1.7 copy.178
  278.8 2.6 stack.92
  283.4 3.6 convolution_bitcast_fusion.2
  287.0 2.3 convolution_bitcast_fusion.3
  289.7 2.6 copy.179
  292.3 20.5 %all-to-all-done.4 = f32[256,1,1280]{2,1,0:T(1,128)} async-done(((f32[256,1,1280]{2,1,0:T(1,128)}), f32[256,1,1280]{2,1,0:T(1,128)}, u32[]{:S(2)}, u32[]{:S(2)}) %all-to-all-start.4) | async-done | bytes 1310752 | tf_op jit(solution)/shard_map/all_to_all | solution.py:96
  312.9 5.2 %all-to-all-start.1 = ((f32[1,96,2,3,768]{4,2,3,0,1:T(2,128)}), f32[1,96,2,3,768]{4,2,3,0,1:T(2,128)S(1)}, u32[]{:S(2)}, u32[]{:S(2)}) async-start(f32[1,96,2,3,768]{4,2,3,0,1:T(2,128)} %copy.179), calls=%async_computation.1 | async-start | bytes 3538944 | tf_op jit(solution)/shard_map/all_to_all | solution.py:137
  318.1 2.1 reduce_sum.89
  320.2 40.4 %all-to-all-done.1 = f32[1,96,2,3,768]{4,2,3,0,1:T(2,128)S(1)} async-done(((f32[1,96,2,3,768]{4,2,3,0,1:T(2,128)}), f32[1,96,2,3,768]{4,2,3,0,1:T(2,128)S(1)}, u32[]{:S(2)}, u32[]{:S(2)}) %all-to-all-start.1) | async-done | bytes 1769504 | tf_op jit(solution)/shard_map/all_to_all | solution.py:137
  360.6 1.8 broadcast_in_dim.12
  362.3 9.7 %all-to-all-start.5 = ((f32[256,1,1280]{2,1,0:T(1,128)}), f32[256,1,1280]{2,1,0:T(1,128)}, u32[]{:S(2)}, u32[]{:S(2)}) async-start(f32[256,1,1280]{2,1,0:T(1,128)} %broadcast_in_dim.12), calls=%async_computation.5 | async-start | bytes 2621440 | tf_op jit(solution)/shard_map/all_to_all | solution.py:98
  372.8 2.8 fusion.32
  375.5 1.6 fusion.30
  377.1 30.8 %all-to-all-done.5 = f32[256,1,1280]{2,1,0:T(1,128)} async-done(((f32[256,1,1280]{2,1,0:T(1,128)}), f32[256,1,1280]{2,1,0:T(1,128)}, u32[]{:S(2)}, u32[]{:S(2)}) %all-to-all-start.5) | async-done | bytes 1310752 | tf_op jit(solution)/shard_map/all_to_all | solution.py:98
  (157 shorter events, 35.0 us)
Async XLA Ops:
  0.6 3.5 copy-start.5
  0.6 3.5 copy-start.47
  0.7 3.5 copy-start.49
  4.1 17.5 %copy-start.36 = (f32[180,1,96]{2,0,1:T(8,128)}, f32[180,1,96]{2,0,1:T(8,128)S(1)}, u32[]{:S(2)}) copy-start(f32[180,1,96]{2,0,1:T(8,128)S(1)} %get-tuple-element.30) | copy-start | bytes 207364
  4.1 17.5 %copy-start.38 = (f32[180,1,96]{2,0,1:T(8,128)}, f32[180,1,96]{2,0,1:T(8,128)S(1)}, u32[]{:S(2)}) copy-start(f32[180,1,96]{2,0,1:T(8,128)S(1)} %get-tuple-element.31) | copy-start | bytes 207364
  8.7 12.9 %copy-start.29 = (bf16[1,3,180,768]{3,2,1,0:T(8,128)(2,1)S(1)}, bf16[1,3,180,768]{3,2,1,0:T(8,128)(2,1)}, u32[]{:S(2)}) copy-start(bf16[1,3,180,768]{3,2,1,0:T(8,128)(2,1)} %param.15) | copy-start | bytes 2488324
  8.7 55.7 %all-to-all-start = ((f32[1,3,2,96,768]{4,2,1,0,3:T(2,128)}), f32[1,3,2,96,768]{4,2,1,0,3:T(2,128)S(1)}, u32[]{:S(2)}, u32[]{:S(2)}) async-start(f32[1,3,2,96,768]{4,2,1,0,3:T(2,128)} %copy.168), calls=%async_computation | async-start | bytes 3538944 | tf_op jit(solution)/shard_map/all_to_all | solution.py:129
  21.6 3.6 copy-start.51
  64.4 50.6 %all-to-all-start.2 = ((f32[1,3,2,96,768]{4,2,1,0,3:T(2,128)}), f32[1,3,2,96,768]{4,2,1,0,3:T(2,128)S(1)}, u32[]{:S(2)}, u32[]{:S(2)}) async-start(f32[1,3,2,96,768]{4,2,1,0,3:T(2,128)} %copy.182), calls=%async_computation.2 | async-start | bytes 3538944 | tf_op jit(solution)/shard_map/all_to_all | solution.py:138
  119.3 3.1 copy-start.23
  124.6 4.9 %copy-start.9 = (f32[2,8,96,96]{3,2,1,0:T(8,128)S(1)}, f32[2,8,96,96]{3,2,1,0:T(8,128)}, u32[]{:S(2)}) copy-start(f32[2,8,96,96]{3,2,1,0:T(8,128)} %param.11) | copy-start | bytes 1769476
  129.6 4.0 copy-start.3
  135.6 2.1 copy-start.15
  135.6 2.1 copy-start.40
  137.7 1.0 copy-start.17
  137.7 1.6 copy-start.7
  139.3 22.4 %copy-start.2 = (f32[1,96,2,3,8,96]{5,1,3,4,2,0:T(8,128)}, f32[1,96,2,3,8,96]{5,1,3,4,2,0:T(8,128)S(1)}, u32[]{:S(2)}) copy-start(f32[1,96,2,3,8,96]{5,1,3,4,2,0:T(8,128)S(1)} %multiply_multiply_fusion.2) | copy-start | bytes 5308420
  139.3 4.4 %copy-start.22 = (f32[1,96,2,3,768]{4,1,3,2,0:T(8,128)S(1)}, f32[1,96,2,3,768]{4,1,3,2,0:T(8,128)}, u32[]{:S(2)}) copy-start(f32[1,96,2,3,768]{4,1,3,2,0:T(8,128)} %fusion.47) | copy-start | bytes 5308420
  141.5 2.2 copy-start.21
  150.7 1.6 copy-start.8
  150.8 1.9 copy-start.28
  152.6 1.3 copy-start.27
  153.9 1.9 copy-start.13
  153.9 1.7 copy-start.26
  155.6 2.8 copy-start.11
  155.6 0.7 copy-start.41
  158.4 10.5 %copy-start = (f32[1,96,2,3,8,96]{5,1,3,4,2,0:T(8,128)}, f32[1,96,2,3,8,96]{5,1,3,4,2,0:T(8,128)S(1)}, u32[]{:S(2)}) copy-start(f32[1,96,2,3,8,96]{5,1,3,4,2,0:T(8,128)S(1)} %get-tuple-element.13) | copy-start | bytes 5308420
  168.9 1.3 copy-start.16
  168.9 1.6 copy-start.18
  170.5 2.6 copy-start.10
  189.0 4.7 %copy-start.19 = (f32[1,96,1,3,768]{4,1,3,2,0:T(8,128)S(1)}, f32[1,96,1,3,768]{4,1,3,2,0:T(8,128)}, u32[]{:S(2)}) copy-start(f32[1,96,1,3,768]{4,1,3,2,0:T(8,128)} %stack.105) | copy-start | bytes 2654212
  189.0 4.7 %copy-start.20 = (f32[1,96,1,3,768]{4,1,3,2,0:T(8,128)S(1)}, f32[1,96,1,3,768]{4,1,3,2,0:T(8,128)}, u32[]{:S(2)}) copy-start(f32[1,96,1,3,768]{4,1,3,2,0:T(8,128)} %stack.104) | copy-start | bytes 2654212
  193.7 3.2 copy-start.44
  197.5 5.2 %copy-start.1 = (f32[1,96,2,3,8,96]{5,1,3,4,2,0:T(8,128)S(1)}, f32[1,96,2,3,8,96]{5,1,3,4,2,0:T(8,128)}, u32[]{:S(2)}) copy-start(f32[1,96,2,3,8,96]{5,1,3,4,2,0:T(8,128)} %copy-done) | copy-start | bytes 5308420
  197.5 9.9 %copy-start.25 = (f32[1,96,2,3,768]{4,1,3,2,0:T(8,128)S(1)}, f32[1,96,2,3,768]{4,1,3,2,0:T(8,128)}, u32[]{:S(2)}) copy-start(f32[1,96,2,3,768]{4,1,3,2,0:T(8,128)} %convolution_bitcast_fusion.1) | copy-start | bytes 5308420
  202.8 4.7 %copy-start.24 = (f32[1,96,2,3,768]{4,1,3,2,0:T(8,128)S(1)}, f32[1,96,2,3,768]{4,1,3,2,0:T(8,128)}, u32[]{:S(2)}) copy-start(f32[1,96,2,3,768]{4,1,3,2,0:T(8,128)} %convolution_bitcast_fusion) | copy-start | bytes 5308420
  210.4 50.0 %all-to-all-start.3 = ((f32[1,96,2,3,768]{4,2,3,0,1:T(2,128)}), f32[1,96,2,3,768]{4,2,3,0,1:T(2,128)}, u32[]{:S(2)}, u32[]{:S(2)}) async-start(f32[1,96,2,3,768]{4,2,3,0,1:T(2,128)} %copy.191), calls=%async_computation.3 | async-start | bytes 3538944 | tf_op jit(solution)/shard_map/all_to_all | solution.py:153
  216.5 4.5 %copy-start.43 = (f32[2,8,96]{2,1,0:T(8,128)S(1)}, f32[2,8,96]{2,1,0:T(8,128)}, u32[]{:S(2)}) copy-start(f32[2,8,96]{2,1,0:T(8,128)} %get-tuple-element.14) | copy-start | bytes 18436
  221.7 3.0 copy-start.4
  229.7 0.7 copy-start.46
  229.7 1.1 copy-start.32
  229.8 1.1 copy-start.45
  260.5 2.2 copy-start.6
  260.5 2.3 copy-start.30
  260.5 2.3 copy-start.37
  260.5 2.3 copy-start.39
  260.5 2.3 copy-start.48
  267.4 9.6 %copy-start.42 = (f32[2,8,96]{2,1,0:T(8,128)S(1)}, f32[2,8,96]{2,1,0:T(8,128)}, u32[]{:S(2)}) copy-start(f32[2,8,96]{2,1,0:T(8,128)} %param.14) | copy-start | bytes 18436
  267.4 9.7 %copy-start.14 = (f32[8,96,3,96]{3,1,2,0:T(8,128)S(1)}, f32[8,96,3,96]{3,1,2,0:T(8,128)}, u32[]{:S(2)}) copy-start(f32[8,96,3,96]{3,1,2,0:T(8,128)} %copy-done.13) | copy-start | bytes 2654212
  267.4 45.5 %all-to-all-start.4 = ((f32[256,1,1280]{2,1,0:T(1,128)}), f32[256,1,1280]{2,1,0:T(1,128)}, u32[]{:S(2)}, u32[]{:S(2)}) async-start(f32[256,1,1280]{2,1,0:T(1,128)} %bitcast.367), calls=%async_computation.4 | async-start | bytes 2621440 | tf_op jit(solution)/shard_map/all_to_all | solution.py:96
  277.1 4.3 %copy-start.12 = (f32[8,96,3,96]{3,1,2,0:T(8,128)S(1)}, f32[8,96,3,96]{3,1,2,0:T(8,128)}, u32[]{:S(2)}) copy-start(f32[8,96,3,96]{3,1,2,0:T(8,128)} %copy-done.11) | copy-start | bytes 2654212
  282.1 1.3 copy-start.34
  283.4 3.6 copy-start.35
  312.9 47.7 %all-to-all-start.1 = ((f32[1,96,2,3,768]{4,2,3,0,1:T(2,128)}), f32[1,96,2,3,768]{4,2,3,0,1:T(2,128)S(1)}, u32[]{:S(2)}, u32[]{:S(2)}) async-start(f32[1,96,2,3,768]{4,2,3,0,1:T(2,128)} %copy.179), calls=%async_computation.1 | async-start | bytes 3538944 | tf_op jit(solution)/shard_map/all_to_all | solution.py:137
  362.3 45.6 %all-to-all-start.5 = ((f32[256,1,1280]{2,1,0:T(1,128)}), f32[256,1,1280]{2,1,0:T(1,128)}, u32[]{:S(2)}, u32[]{:S(2)}) async-start(f32[256,1,1280]{2,1,0:T(1,128)} %broadcast_in_dim.12), calls=%async_computation.5 | async-start | bytes 2621440 | tf_op jit(solution)/shard_map/all_to_all | solution.py:98
  372.1 0.7 copy-start.50
  372.1 0.7 copy-start.52
  372.8 2.8 copy-start.31
  372.8 2.8 copy-start.33

commit v2 on v1

--- a/solution.py
+++ b/solution.py
@@ -104,6 +104,22 @@
     return tuple(results)
 
 
+def lat_in(values_in, cosine_in, sine_in, orient):
+    cosine_part = jnp.einsum("pjh,jshrmc->sprmc", cosine_in, values_in, precision=HIGHEST)
+    sine_part = jnp.einsum("pjh,jshrmc->sprmc", sine_in, values_in, precision=HIGHEST)
+    real_part = cosine_part[:, :, 0] + orient * sine_part[:, :, 1]
+    imag_part = cosine_part[:, :, 1] - orient * sine_part[:, :, 0]
+    return jnp.stack([real_part, imag_part], axis=2)
+
+
+def lat_out(values_in, cosine_out, sine_out, orient):
+    cosine_part = jnp.einsum("jih,shrmc->jsirmc", cosine_out, values_in, precision=HIGHEST)
+    sine_part = jnp.einsum("jih,shrmc->jsirmc", sine_out, values_in, precision=HIGHEST)
+    real_part = cosine_part[:, :, :, 0] + orient * sine_part[:, :, :, 1]
+    imag_part = cosine_part[:, :, :, 1] - orient * sine_part[:, :, :, 0]
+    return jnp.stack([real_part, imag_part], axis=3)
+
+
 def local(tokens, norm_gain, norm_shift, weight_one, bias_one, weight_two, bias_two, cotangent):
     lat_parts = lax.axis_size("lat")
     samples, local_rows, lon_cells, features = tokens.shape
@@ -112,9 +128,16 @@
     lat_rows = local_rows * lat_parts
     kept_modes = lon_cells // 2 + 1
     padded = (kept_modes + lat_parts - 1) // lat_parts * lat_parts
+    local_modes = padded // lat_parts
     lon_table = lon_basis(lon_cells, padded)
     weighted = lon_table * lon_weight(lon_cells, padded)[None, None, :]
+    lon_blocks = lon_table.reshape(lon_cells, 2, lat_parts, local_modes)
+    weighted_blocks = weighted.reshape(lon_cells, 2, lat_parts, local_modes)
     cosine, sine_table = lat_basis(lat_rows)
+    cosine_in = cosine.reshape(lat_rows, lat_parts, local_rows)
+    sine_in = sine_table.reshape(lat_rows, lat_parts, local_rows)
+    cosine_out = cosine.reshape(lat_parts, local_rows, lat_rows)
+    sine_out = sine_table.reshape(lat_parts, local_rows, lat_rows)
     float_tokens = tokens.astype(jnp.float32)
     average = jnp.mean(float_tokens, axis=-1, keepdims=True)
     centred = float_tokens - average
@@ -123,38 +146,35 @@
     normalized = centred * inverse_std
     normed = normalized * norm_gain + norm_shift
     upstream_out = cotangent.astype(jnp.float32)
-    lon_spectrum = jnp.einsum("shwc,wrk->shrkc", normed, lon_table, precision=HIGHEST)
-    cotangent_lon = jnp.einsum("shwc,wrk->shrkc", upstream_out, weighted, precision=HIGHEST)
-    mode_shape = (samples, lat_rows, 2, padded // lat_parts, groups, block_size)
-    gathered = lax.all_to_all(lon_spectrum, "lat", split_axis=3, concat_axis=1, tiled=True)
-    spectrum = lat_apply(gathered, cosine, sine_table, 1.0).reshape(mode_shape)
+    lon_spectrum = jnp.einsum("shwc,wrjm->jshrmc", normed, lon_blocks, precision=HIGHEST)
+    cotangent_lon = jnp.einsum("shwc,wrjm->jshrmc", upstream_out, weighted_blocks, precision=HIGHEST)
+    leaving_modes = jnp.concatenate([lon_spectrum, cotangent_lon], axis=3)
+    arrived = lax.all_to_all(leaving_modes, "lat", 0, 0, tiled=True)
+    mode_shape = (samples, lat_rows, 2, local_modes, groups, block_size)
+    row_shape = (samples, lat_rows, 2, local_modes, features)
+    spectrum = lat_in(arrived[:, :, :, :2], cosine_in, sine_in, 1.0).reshape(mode_shape)
     pre_inner = block_product(spectrum, weight_one) + bias_one[None, None, :, None]
     inner_act, gelu_back = jax.vjp(jax.nn.gelu, pre_inner)
     pre_outer = block_product(inner_act, weight_two) + bias_two[None, None, :, None]
     shrunk, shrink_back = jax.vjp(shrink, pre_outer)
-    leaving = lat_apply(shrunk.reshape(gathered.shape), cosine, sine_table, -1.0)
-    leaving, saved_state = (leaving, (spectrum, inner_act, gelu_back, shrink_back))
-    returned = lax.all_to_all(leaving, "lat", split_axis=1, concat_axis=3, tiled=True)
-    cotangent_modes = lax.all_to_all(cotangent_lon, "lat", split_axis=3, concat_axis=1, tiled=True)
-    spectrum, inner_act, gelu_back, shrink_back = saved_state
-    shrunk_grad = lat_apply(cotangent_modes, cosine, sine_table, 1.0).reshape(mode_shape)
+    leaving = lat_out(shrunk.reshape(row_shape), cosine_out, sine_out, -1.0)
+    shrunk_grad = lat_in(arrived[:, :, :, 2:], cosine_in, sine_in, 1.0).reshape(mode_shape)
     outer_grad = shrink_back(shrunk_grad)[0]
     weight_two_grad = weight_grad(inner_act, outer_grad)
     bias_two_grad = jnp.sum(outer_grad, axis=(0, 1, 3))
     inner_grad = gelu_back(block_adjoint(outer_grad, weight_two))[0]
     weight_one_grad = weight_grad(spectrum, inner_grad)
     bias_one_grad = jnp.sum(inner_grad, axis=(0, 1, 3))
-    spectrum_grad = block_adjoint(inner_grad, weight_one).reshape(cotangent_modes.shape)
-    adjoint_modes = lat_apply(spectrum_grad, cosine, sine_table, -1.0)
-    adjoint_modes, spectral_grads = (
-        adjoint_modes,
-        (weight_one_grad, bias_one_grad, weight_two_grad, bias_two_grad),
-    )
-    adjoint_rows = lax.all_to_all(adjoint_modes, "lat", split_axis=1, concat_axis=3, tiled=True)
-    filtered = jnp.einsum("shrkc,wrk->shwc", returned, weighted, precision=HIGHEST)
+    spectrum_grad = block_adjoint(inner_grad, weight_one).reshape(row_shape)
+    adjoint_modes = lat_out(spectrum_grad, cosine_out, sine_out, -1.0)
+    leaving_rows = jnp.concatenate([leaving, adjoint_modes], axis=3)
+    returned = lax.all_to_all(leaving_rows, "lat", 0, 0, tiled=True)
+    filtered = jnp.einsum(
+        "jshrmc,wrjm->shwc", returned[:, :, :, :2], weighted_blocks, precision=HIGHEST
+    )
     block_out = (float_tokens + normed + filtered).astype(jnp.bfloat16)
     normed_grad = upstream_out + jnp.einsum(
-        "shrkc,wrk->shwc", adjoint_rows, lon_table, precision=HIGHEST
+        "jshrmc,wrjm->shwc", returned[:, :, :, 2:], lon_blocks, precision=HIGHEST
     )
     hat_grad = normed_grad * norm_gain
     hat_mean = jnp.mean(hat_grad, axis=-1, keepdims=True)
@@ -164,10 +184,10 @@
     local_shift = jnp.sum(normed_grad, axis=(0, 1, 2))
     summed = flat_sum(
         (
-            spectral_grads[0],
-            spectral_grads[1],
-            spectral_grads[2],
-            spectral_grads[3],
+            weight_one_grad,
+            bias_one_grad,
+            weight_two_grad,
+            bias_two_grad,
             local_gain,
             local_shift,
         ),

time: 423 us -> 414 us (0.979)
  blocking collectives: 0 us -> 45.3 us
  waiting for transfers between devices: 198 us -> 160 us
  starting transfers between devices: 50.3 us -> 24.6 us
  local copies, waits for them, and re-layouts: 61.4 us -> 74.4 us
    all_to_all x0 -> x1, blocking collectives: none -> 45.3 us  [flat_sum(): reduced = lax.all_to_all(flat, axes, 0, 0, tiled=True).sum(axis=0)]
    all_to_all x5 -> x2, waiting for transfers between devices: 167 us -> 129 us  [the longest x1 81.1 us: local(): arrived = lax.all_to_all(leaving_modes, 'lat', 0, 0, tiled=True)]
    all_to_all x5 -> x2, starting transfers between devices: 40.6 us -> 18.9 us  [the longest x1 13.1 us: local(): arrived = lax.all_to_all(leaving_modes, 'lat', 0, 0, tiled=True)]
    slice x0 -> x2, local copies, waits for them, and re-layouts: none -> 10.4 us  [the longest x1 5.84 us: local(): returned[:, :, :, 2:]]
    concatenate x0 -> x2, local copies, waits for them, and re-layouts: none -> 8.23 us  [the longest x1 4.16 us: local(): leaving_rows = jnp.concatenate([leaving, adjoint_modes], axis=3)]
    unnamed x112 -> x110, local copies, waits for them, and re-layouts: 4.89 us -> 10.8 us
    another operation x9 -> x7, local copies, waits for them, and re-layouts: 16.8 us -> 11.1 us  [the longest x3 5.66 us: lat_in(): return jnp.stack([real_part, imag_part], axis=2)]
    all_to_all x6 -> x0, local copies, waits for them, and re-layouts: 5.26 us -> none  [the longest x1 2.22 us: local(): lax.all_to_all(adjoint_modes, 'lat', split_axis=1, concat_axis=3, tiled=T...]
  transfers between devices with their start and end apart: 6 -> 3, of which waited for: 6 -> 3; matrix products, arithmetic and copies ran while one was open for 11% -> 10% of each run, Pallas kernels for 0% -> 0%
where the time goes in v2:
time: 414 us; the launch traced here: 407 us
  waiting for transfers between devices  160 us (39%)
  matrix products  82.8 us (20%)
  local copies, waits for them, and re-layouts  74.4 us (18%)
  blocking collectives  45.3 us (11%)
  starting transfers between devices  24.6 us (6%)
  other arithmetic  18.4 us (4%)
    all_to_all x1, waiting for transfers between devices, local(): arrived = lax.all_to_all(leaving_modes, 'lat', 0, 0, tiled=True)  81.1 us
    all_to_all x1, waiting for transfers between devices, local(): returned = lax.all_to_all(leaving_rows, 'lat', 0, 0, tiled=True)  48.3 us
    all_to_all x1, blocking collectives, flat_sum(): reduced = lax.all_to_all(flat, axes, 0, 0, tiled=True).sum(axis=0)  45.3 us
    all_to_all x1, waiting for transfers between devices, flat_sum(): whole = lax.all_to_all(spread, axes, 0, 0, tiled=True).reshape(-1)  30.6 us
    dot_general x8, matrix products, contract(): jnp.einsum('shkgi,shkgo->gio', left_side, right_side, precision=HIGHEST)  21.4 us
    dot_general x8, matrix products, product_part(): jnp.einsum('shkgi,gio->shkgo', part_in, weights[slot_index], precision=HI...  15.4 us
    all_to_all x1, starting transfers between devices, local(): arrived = lax.all_to_all(leaving_modes, 'lat', 0, 0, tiled=True)  13.1 us
    dot_general x8, matrix products, product_part(): jnp.einsum('shkgo,gio->shkgi', part_in, weights[slot_index], precision=HI...  12.1 us
  transfers between devices with their start and end apart: 3, of which 3 were waited for; matrix products, arithmetic and copies ran while one was open for 10% of the time, Pallas kernels for 0%

profile of v2, /device:TPU:1, one launch (start us, length us, event | category | flops | bytes accessed | tf_op | source)
XLA Modules:
  0.0 407.3 jit_solution(13886507164237452059)
XLA Ops:
  0.7 1.4 convert_reduce_fusion
  2.2 1.6 fusion.31
  5.3 1.9 fusion.43
  7.6 4.1 copy.126
  11.6 13.1 %all-to-all-start = ((f32[32,1,3,4,3,768]{5,3,4,2,1,0:T(4,128)}), f32[32,1,3,4,3,768]{5,3,4,2,1,0:T(4,128)}, u32[]{:S(2)}, u32[]{:S(2)}) async-start(f32[32,1,3,4,3,768]{5,3,4,2,1,0:T(4,128)} %copy.126), calls=%async_computation | async-start | bytes 7077888 | tf_op jit(solution)/shard_map/all_to_all | solution.py:152
  25.5 81.1 %all-to-all-done = f32[32,1,3,4,3,768]{5,3,4,2,1,0:T(4,128)} async-done(((f32[32,1,3,4,3,768]{5,3,4,2,1,0:T(4,128)}), f32[32,1,3,4,3,768]{5,3,4,2,1,0:T(4,128)}, u32[]{:S(2)}, u32[]{:S(2)}) %all-to-all-start) | async-done | bytes 3538976 | tf_op jit(solution)/shard_map/all_to_all | solution.py:152
  106.6 4.6 %fusion.254 = (f32[32,1,3,2,3,768]{5,3,4,2,1,0:T(2,128)S(1)}, f32[32,1,3,2,3,768]{5,3,4,2,1,0:T(2,128)S(1)}) fusion(f32[32,1,3,4,3,768]{5,3,4,2,1,0:T(4,128)} %all-to-all-done), kind=kLoop, calls=%fused_computation.320 | loop fusion | bytes 7077888 | tf_op jit(solution)/shard_map/slice | solution.py:161
  111.2 3.2 fusion.40
  114.4 3.2 fusion.39
  117.6 2.0 fusion.42
  119.6 2.0 fusion.41
  123.8 2.8 reshape.937
  126.7 1.6 copy.143
  128.3 2.4 fusion.97
  130.8 2.0 fusion.95
  132.8 2.0 fusion.52
  134.8 2.0 fusion.53
  138.5 2.2 fusion.67
  140.6 2.2 fusion.66
  142.8 1.5 slice_subtract_fusion
  144.3 2.7 stack.89
  147.1 2.7 stack.88
  149.8 1.8 copy_dynamic-update-slice_fusion.1
  155.4 2.1 fusion.249
  162.8 2.6 fusion.251
  166.6 2.3 fusion.70
  170.1 1.7 copy.138
  171.8 2.6 stack.98
  174.4 2.6 fusion.56
  177.0 1.8 copy.137
  178.8 2.6 stack.97
  181.4 4.8 %convolution_bitcast_fusion = f32[32,1,3,2,3,768]{5,0,2,4,3,1:T(8,128)} fusion(f32[1,96,1,3,768]{4,1,3,2,0:T(8,128)} %stack.98, f32[1,96,1,3,768]{4,1,3,2,0:T(8,128)} %stack.97, s32[32,3]{0,1:T(4,128)S(1)} %multiply_add_fusion), kind=kOutput, calls=%fused_computation.68 | convolution fusion | flops 510142464 | bytes 3539328 | tf_op jit(solution)/shard_map/jih,shrmc->jsirmc/dot_general | solution.py:117
  186.3 3.2 convolution_bitcast_fusion.1
  189.5 1.7 copy.133
  191.2 2.6 stack.86
  193.8 3.4 copy.132
  197.1 2.6 stack.85
  199.7 4.0 fusion.49
  203.7 2.4 fusion.46
  207.3 4.2 %copy.139 = f32[32,1,3,4,3,768]{5,3,4,2,1,0:T(4,128)} copy(f32[32,1,3,4,3,768]{5,0,2,4,3,1:T(8,128)S(1)} %pad_maximum_fusion.1) | data formatting | bytes 7077888 | tf_op jit(solution)/shard_map/concatenate | solution.py:170
  211.5 5.8 %all-to-all-start.1 = ((f32[32,1,3,4,3,768]{5,3,4,2,1,0:T(4,128)}), f32[32,1,3,4,3,768]{5,3,4,2,1,0:T(4,128)}, u32[]{:S(2)}, u32[]{:S(2)}) async-start(f32[32,1,3,4,3,768]{5,3,4,2,1,0:T(4,128)} %copy.139), calls=%async_computation.1 | async-start | bytes 7077888 | tf_op jit(solution)/shard_map/all_to_all | solution.py:171
  217.3 1.4 reshape.951
  218.6 4.3 %convolution_bitcast_fusion.5 = f32[8,96,96]{2,1,0:T(8,128)S(1)} fusion(f32[1,96,2,3,8,96]{5,1,3,4,2,0:T(8,128)} %copy-done.2, f32[1,96,2,3,8,96]{5,1,3,4,2,0:T(8,128)} %copy-done), kind=kOutput, calls=%fused_computation.88 | convolution fusion | flops 254803968 | bytes 2654208 | tf_op jit(solution)/shard_map/shkgi,shkgo->gio/dot_general | solution.py:73
  222.9 3.9 convolution_bitcast_fusion.3
  226.8 2.5 fusion.63
  229.3 2.5 fusion.65
  232.8 2.4 reshape.950
  235.2 1.4 reshape.949
  236.6 3.0 convolution_bitcast_fusion.9
  239.6 1.9 convolution_bitcast_fusion.7
  241.5 1.6 fusion.61
  243.1 1.6 fusion.59
  246.2 1.3 constant_dynamic-update-slice_fusion.5
  247.5 2.0 constant_dynamic-update-slice_fusion.4
  250.8 48.3 %all-to-all-done.1 = f32[32,1,3,4,3,768]{5,3,4,2,1,0:T(4,128)} async-done(((f32[32,1,3,4,3,768]{5,3,4,2,1,0:T(4,128)}), f32[32,1,3,4,3,768]{5,3,4,2,1,0:T(4,128)}, u32[]{:S(2)}, u32[]{:S(2)}) %all-to-all-start.1) | async-done | bytes 3538976 | tf_op jit(solution)/shard_map/all_to_all | solution.py:171
  299.1 5.8 %fusion.253 = (f32[32,1,3,2,3,768]{5,3,4,2,1,0:T(2,128)S(1)}, f32[32,1,3,2,3,768]{5,3,4,2,1,0:T(2,128)}) fusion(f32[32,1,3,4,3,768]{5,3,4,2,1,0:T(4,128)} %all-to-all-done.1), kind=kLoop, calls=%fused_computation.319 | loop fusion | bytes 7077888 | tf_op jit(solution)/shard_map/slice | solution.py:177
  305.0 3.4 fusion.30
  310.9 1.4 pad.4
  312.3 45.3 %all_to_all.25 = f32[256,1,1280]{2,1,0:T(1,128)S(1)} all-to-all(f32[256,1,1280]{2,1,0:T(1,128)S(1)} %bitcast.424), channel_id=1, replica_groups=mesh['sample'=8,'lat'=32] {'sample','lat'}, dimensions={0} | all-to-all | bytes 2621440 | tf_op jit(solution)/shard_map/all_to_all | solution.py:96
  358.4 1.8 broadcast_in_dim.12
  360.2 5.7 %all-to-all-start.3 = ((f32[256,1,1280]{2,1,0:T(1,128)}), f32[256,1,1280]{2,1,0:T(1,128)S(1)}, u32[]{:S(2)}, u32[]{:S(2)}) async-start(f32[256,1,1280]{2,1,0:T(1,128)} %broadcast_in_dim.12), calls=%async_computation.3 | async-start | bytes 2621440 | tf_op jit(solution)/shard_map/all_to_all | solution.py:98
  366.0 3.2 fusion.32
  369.2 2.9 fusion.34
  372.1 30.6 %all-to-all-done.3 = f32[256,1,1280]{2,1,0:T(1,128)S(1)} async-done(((f32[256,1,1280]{2,1,0:T(1,128)}), f32[256,1,1280]{2,1,0:T(1,128)S(1)}, u32[]{:S(2)}, u32[]{:S(2)}) %all-to-all-start.3) | async-done | bytes 1310752 | tf_op jit(solution)/shard_map/all_to_all | solution.py:98
  (145 shorter events, 30.1 us)
Async XLA Ops:
  0.6 3.7 copy-start.28
  2.1 3.2 copy-start.6
  2.1 3.2 copy-start.47
  2.1 3.2 copy-start.50
  4.3 0.9 copy-start.33
  4.3 0.9 copy-start.36
  11.6 13.1 %copy-start.43 = (f32[2,8,96]{2,1,0:T(8,128)S(1)}, f32[2,8,96]{2,1,0:T(8,128)}, u32[]{:S(2)}) copy-start(f32[2,8,96]{2,1,0:T(8,128)} %param.14) | copy-start | bytes 18436
  11.6 94.9 %all-to-all-start = ((f32[32,1,3,4,3,768]{5,3,4,2,1,0:T(4,128)}), f32[32,1,3,4,3,768]{5,3,4,2,1,0:T(4,128)}, u32[]{:S(2)}, u32[]{:S(2)}) async-start(f32[32,1,3,4,3,768]{5,3,4,2,1,0:T(4,128)} %copy.126), calls=%async_computation | async-start | bytes 7077888 | tf_op jit(solution)/shard_map/all_to_all | solution.py:152
  123.8 4.5 %copy-start.10 = (f32[2,8,96,96]{3,2,1,0:T(8,128)S(1)}, f32[2,8,96,96]{3,2,1,0:T(8,128)}, u32[]{:S(2)}) copy-start(f32[2,8,96,96]{3,2,1,0:T(8,128)} %param.11) | copy-start | bytes 1769476
  128.3 4.5 %copy-start.4 = (f32[96,3,8,96]{0,3,1,2:T(8,128)}, f32[96,3,8,96]{0,3,1,2:T(8,128)S(1)}, u32[]{:S(2)}) copy-start(f32[96,3,8,96]{0,3,1,2:T(8,128)S(1)} %copy.143) | copy-start | bytes 2654212
  134.8 2.1 copy-start.15
  134.8 2.1 copy-start.41
  136.9 1.1 copy-start.17
  136.9 1.6 copy-start.8
  138.5 14.5 %copy-start.2 = (f32[1,96,2,3,8,96]{5,1,3,4,2,0:T(8,128)}, f32[1,96,2,3,8,96]{5,1,3,4,2,0:T(8,128)S(1)}, u32[]{:S(2)}) copy-start(f32[1,96,2,3,8,96]{5,1,3,4,2,0:T(8,128)S(1)} %multiply_multiply_fusion.2) | copy-start | bytes 5308420
  138.5 4.4 %copy-start.22 = (f32[1,96,2,3,768]{4,1,3,2,0:T(8,128)S(1)}, f32[1,96,2,3,768]{4,1,3,2,0:T(8,128)}, u32[]{:S(2)}) copy-start(f32[1,96,2,3,768]{4,1,3,2,0:T(8,128)} %fusion.39) | copy-start | bytes 5308420
  140.6 2.2 copy-start.21
  149.8 1.8 copy-start.9
  149.8 1.9 copy-start.27
  151.7 1.3 copy-start.26
  153.0 1.9 copy-start.13
  153.0 1.7 copy-start.25
  154.7 2.8 copy-start.12
  154.7 0.7 copy-start.44
  157.5 3.6 copy-start
  161.2 1.3 copy-start.16
  161.2 1.6 copy-start.18
  161.2 1.6 copy-start.42
  162.8 2.6 copy-start.11
  181.4 4.8 %copy-start.19 = (f32[1,96,1,3,768]{4,1,3,2,0:T(8,128)S(1)}, f32[1,96,1,3,768]{4,1,3,2,0:T(8,128)}, u32[]{:S(2)}) copy-start(f32[1,96,1,3,768]{4,1,3,2,0:T(8,128)} %stack.98) | copy-start | bytes 2654212
  181.4 4.8 %copy-start.20 = (f32[1,96,1,3,768]{4,1,3,2,0:T(8,128)S(1)}, f32[1,96,1,3,768]{4,1,3,2,0:T(8,128)}, u32[]{:S(2)}) copy-start(f32[1,96,1,3,768]{4,1,3,2,0:T(8,128)} %stack.97) | copy-start | bytes 2654212
  186.3 3.2 copy-start.14
  199.7 4.0 copy-start.39
  199.7 4.0 copy-start.40
  199.7 4.0 copy-start.49
  203.7 2.4 copy-start.23
  203.7 2.4 copy-start.24
  211.5 87.6 %all-to-all-start.1 = ((f32[32,1,3,4,3,768]{5,3,4,2,1,0:T(4,128)}), f32[32,1,3,4,3,768]{5,3,4,2,1,0:T(4,128)}, u32[]{:S(2)}, u32[]{:S(2)}) async-start(f32[32,1,3,4,3,768]{5,3,4,2,1,0:T(4,128)} %copy.139), calls=%async_computation.1 | async-start | bytes 7077888 | tf_op jit(solution)/shard_map/all_to_all | solution.py:171
  218.6 4.3 %copy-start.1 = (f32[1,96,2,3,8,96]{5,1,3,4,2,0:T(8,128)S(1)}, f32[1,96,2,3,8,96]{5,1,3,4,2,0:T(8,128)}, u32[]{:S(2)}) copy-start(f32[1,96,2,3,8,96]{5,1,3,4,2,0:T(8,128)} %copy-done) | copy-start | bytes 5308420
  222.9 3.9 copy-start.3
  236.6 3.0 copy-start.5
  244.8 1.4 copy-start.46
  244.8 2.7 copy-start.31
  244.9 4.6 %copy-start.45 = (f32[1536]{0:T(1024)S(1)}, f32[1536]{0:T(1024)}, u32[]{:S(2)}) copy-start(f32[1536]{0:T(1024)} %reshape.951) | copy-start | bytes 18436
  250.8 54.1 %copy-start.7 = (bf16[1,3,180,768]{3,2,1,0:T(8,128)(2,1)S(1)}, bf16[1,3,180,768]{3,2,1,0:T(8,128)(2,1)}, u32[]{:S(2)}) copy-start(bf16[1,3,180,768]{3,2,1,0:T(8,128)(2,1)} %param.8) | copy-start | bytes 2488324
  250.8 54.1 %copy-start.29 = (bf16[1,3,180,768]{3,2,1,0:T(8,128)(2,1)S(1)}, bf16[1,3,180,768]{3,2,1,0:T(8,128)(2,1)}, u32[]{:S(2)}) copy-start(bf16[1,3,180,768]{3,2,1,0:T(8,128)(2,1)} %param.15) | copy-start | bytes 2488324
  250.8 54.1 %copy-start.48 = (f32[768]{0:T(1024)S(1)}, f32[768]{0:T(1024)}, u32[]{:S(2)}) copy-start(f32[768]{0:T(1024)} %param.9) | copy-start | bytes 9220
  299.1 5.9 %copy-start.34 = (f32[180,1,32,3]{0,2,3,1:T(8,128)S(1)}, f32[180,1,32,3]{0,2,3,1:T(8,128)}, u32[]{:S(2)}) copy-start(f32[180,1,32,3]{0,2,3,1:T(8,128)} %copy-done.33) | copy-start | bytes 207364
  299.1 5.9 %copy-start.37 = (f32[180,1,32,3]{0,2,3,1:T(8,128)S(1)}, f32[180,1,32,3]{0,2,3,1:T(8,128)}, u32[]{:S(2)}) copy-start(f32[180,1,32,3]{0,2,3,1:T(8,128)} %copy-done.36) | copy-start | bytes 207364
  358.4 7.5 %copy-start.30 = (bf16[1,3,180,768]{3,2,1,0:T(8,128)(2,1)S(1)}, bf16[1,3,180,768]{3,2,1,0:T(8,128)(2,1)}, u32[]{:S(2)}) copy-start(bf16[1,3,180,768]{3,2,1,0:T(8,128)(2,1)} %param.15) | copy-start | bytes 2488324
  360.2 42.5 %all-to-all-start.3 = ((f32[256,1,1280]{2,1,0:T(1,128)}), f32[256,1,1280]{2,1,0:T(1,128)S(1)}, u32[]{:S(2)}, u32[]{:S(2)}) async-start(f32[256,1,1280]{2,1,0:T(1,128)} %broadcast_in_dim.12), calls=%async_computation.3 | async-start | bytes 2621440 | tf_op jit(solution)/shard_map/all_to_all | solution.py:98
  365.9 3.2 copy-start.32
  365.9 3.2 copy-start.35
  365.9 3.2 copy-start.38
  366.0 3.2 copy-start.51

commit v3 on v2

--- a/solution.py
+++ b/solution.py
@@ -105,19 +105,48 @@
 
 
 def lat_in(values_in, cosine_in, sine_in, orient):
-    cosine_part = jnp.einsum("pjh,jshrmc->sprmc", cosine_in, values_in, precision=HIGHEST)
-    sine_part = jnp.einsum("pjh,jshrmc->sprmc", sine_in, values_in, precision=HIGHEST)
+    cosine_part = jnp.einsum("pjh,jshmrc->sprmc", cosine_in, values_in, precision=HIGHEST)
+    sine_part = jnp.einsum("pjh,jshmrc->sprmc", sine_in, values_in, precision=HIGHEST)
     real_part = cosine_part[:, :, 0] + orient * sine_part[:, :, 1]
     imag_part = cosine_part[:, :, 1] - orient * sine_part[:, :, 0]
     return jnp.stack([real_part, imag_part], axis=2)
 
 
 def lat_out(values_in, cosine_out, sine_out, orient):
-    cosine_part = jnp.einsum("jih,shrmc->jsirmc", cosine_out, values_in, precision=HIGHEST)
-    sine_part = jnp.einsum("jih,shrmc->jsirmc", sine_out, values_in, precision=HIGHEST)
-    real_part = cosine_part[:, :, :, 0] + orient * sine_part[:, :, :, 1]
-    imag_part = cosine_part[:, :, :, 1] - orient * sine_part[:, :, :, 0]
-    return jnp.stack([real_part, imag_part], axis=3)
+    cosine_part = jnp.einsum("jih,shrmc->jsimrc", cosine_out, values_in, precision=HIGHEST)
+    sine_part = jnp.einsum("jih,shrmc->jsimrc", sine_out, values_in, precision=HIGHEST)
+    real_part = cosine_part[:, :, :, :, 0] + orient * sine_part[:, :, :, :, 1]
+    imag_part = cosine_part[:, :, :, :, 1] - orient * sine_part[:, :, :, :, 0]
+    return jnp.stack([real_part, imag_part], axis=4)
+
+
+def chunk_spectral(arrived, tables, weights):
+    cosine_in, sine_in, cosine_out, sine_out = tables
+    weight_one, bias_one, weight_two, bias_two = weights
+    samples = arrived.shape[1]
+    local_modes = arrived.shape[3]
+    lat_rows = cosine_in.shape[0]
+    groups = weight_one.shape[1]
+    block_size = weight_one.shape[2]
+    mode_shape = (samples, lat_rows, 2, local_modes, groups, block_size)
+    row_shape = (samples, lat_rows, 2, local_modes, groups * block_size)
+    spectrum = lat_in(arrived[:, :, :, :, :2], cosine_in, sine_in, 1.0).reshape(mode_shape)
+    pre_inner = block_product(spectrum, weight_one) + bias_one[None, None, :, None]
+    inner_act, gelu_back = jax.vjp(jax.nn.gelu, pre_inner)
+    pre_outer = block_product(inner_act, weight_two) + bias_two[None, None, :, None]
+    shrunk, shrink_back = jax.vjp(shrink, pre_outer)
+    leaving = lat_out(shrunk.reshape(row_shape), cosine_out, sine_out, -1.0)
+    shrunk_grad = lat_in(arrived[:, :, :, :, 2:], cosine_in, sine_in, 1.0).reshape(mode_shape)
+    outer_grad = shrink_back(shrunk_grad)[0]
+    weight_two_grad = weight_grad(inner_act, outer_grad)
+    bias_two_grad = jnp.sum(outer_grad, axis=(0, 1, 3))
+    inner_grad = gelu_back(block_adjoint(outer_grad, weight_two))[0]
+    weight_one_grad = weight_grad(spectrum, inner_grad)
+    bias_one_grad = jnp.sum(inner_grad, axis=(0, 1, 3))
+    spectrum_grad = block_adjoint(inner_grad, weight_one).reshape(row_shape)
+    adjoint_modes = lat_out(spectrum_grad, cosine_out, sine_out, -1.0)
+    leaving_rows = jnp.concatenate([leaving, adjoint_modes], axis=4)
+    return leaving_rows, (weight_one_grad, bias_one_grad, weight_two_grad, bias_two_grad)
 
 
 def local(tokens, norm_gain, norm_shift, weight_one, bias_one, weight_two, bias_two, cotangent):
@@ -125,6 +154,9 @@
     samples, local_rows, lon_cells, features = tokens.shape
     groups = weight_one.shape[1]
     block_size = weight_one.shape[2]
+    chunks = 2 if groups % 2 == 0 else 1
+    chunk_groups = groups // chunks
+    chunk_width = chunk_groups * block_size
     lat_rows = local_rows * lat_parts
     kept_modes = lon_cells // 2 + 1
     padded = (kept_modes + lat_parts - 1) // lat_parts * lat_parts
@@ -134,10 +166,12 @@
     lon_blocks = lon_table.reshape(lon_cells, 2, lat_parts, local_modes)
     weighted_blocks = weighted.reshape(lon_cells, 2, lat_parts, local_modes)
     cosine, sine_table = lat_basis(lat_rows)
-    cosine_in = cosine.reshape(lat_rows, lat_parts, local_rows)
-    sine_in = sine_table.reshape(lat_rows, lat_parts, local_rows)
-    cosine_out = cosine.reshape(lat_parts, local_rows, lat_rows)
-    sine_out = sine_table.reshape(lat_parts, local_rows, lat_rows)
+    tables = (
+        cosine.reshape(lat_rows, lat_parts, local_rows),
+        sine_table.reshape(lat_rows, lat_parts, local_rows),
+        cosine.reshape(lat_parts, local_rows, lat_rows),
+        sine_table.reshape(lat_parts, local_rows, lat_rows),
+    )
     float_tokens = tokens.astype(jnp.float32)
     average = jnp.mean(float_tokens, axis=-1, keepdims=True)
     centred = float_tokens - average
@@ -146,62 +180,69 @@
     normalized = centred * inverse_std
     normed = normalized * norm_gain + norm_shift
     upstream_out = cotangent.astype(jnp.float32)
-    lon_spectrum = jnp.einsum("shwc,wrjm->jshrmc", normed, lon_blocks, precision=HIGHEST)
-    cotangent_lon = jnp.einsum("shwc,wrjm->jshrmc", upstream_out, weighted_blocks, precision=HIGHEST)
-    leaving_modes = jnp.concatenate([lon_spectrum, cotangent_lon], axis=3)
-    arrived = lax.all_to_all(leaving_modes, "lat", 0, 0, tiled=True)
-    mode_shape = (samples, lat_rows, 2, local_modes, groups, block_size)
-    row_shape = (samples, lat_rows, 2, local_modes, features)
-    spectrum = lat_in(arrived[:, :, :, :2], cosine_in, sine_in, 1.0).reshape(mode_shape)
-    pre_inner = block_product(spectrum, weight_one) + bias_one[None, None, :, None]
-    inner_act, gelu_back = jax.vjp(jax.nn.gelu, pre_inner)
-    pre_outer = block_product(inner_act, weight_two) + bias_two[None, None, :, None]
-    shrunk, shrink_back = jax.vjp(shrink, pre_outer)
-    leaving = lat_out(shrunk.reshape(row_shape), cosine_out, sine_out, -1.0)
-    shrunk_grad = lat_in(arrived[:, :, :, 2:], cosine_in, sine_in, 1.0).reshape(mode_shape)
-    outer_grad = shrink_back(shrunk_grad)[0]
-    weight_two_grad = weight_grad(inner_act, outer_grad)
-    bias_two_grad = jnp.sum(outer_grad, axis=(0, 1, 3))
-    inner_grad = gelu_back(block_adjoint(outer_grad, weight_two))[0]
-    weight_one_grad = weight_grad(spectrum, inner_grad)
-    bias_one_grad = jnp.sum(inner_grad, axis=(0, 1, 3))
-    spectrum_grad = block_adjoint(inner_grad, weight_one).reshape(row_shape)
-    adjoint_modes = lat_out(spectrum_grad, cosine_out, sine_out, -1.0)
-    leaving_rows = jnp.concatenate([leaving, adjoint_modes], axis=3)
-    returned = lax.all_to_all(leaving_rows, "lat", 0, 0, tiled=True)
-    filtered = jnp.einsum(
-        "jshrmc,wrjm->shwc", returned[:, :, :, :2], weighted_blocks, precision=HIGHEST
-    )
+    arrivals = []
+    for index in range(chunks):
+        cut = slice(index * chunk_width, (index + 1) * chunk_width)
+        lon_spectrum = jnp.einsum(
+            "shwc,wrjm->jshmrc", normed[..., cut], lon_blocks, precision=HIGHEST
+        )
+        cotangent_lon = jnp.einsum(
+            "shwc,wrjm->jshmrc", upstream_out[..., cut], weighted_blocks, precision=HIGHEST
+        )
+        leaving_modes = jnp.concatenate([lon_spectrum, cotangent_lon], axis=4)
+        arrivals.append(lax.all_to_all(leaving_modes, "lat", 0, 0, tiled=True))
+    filtered_parts = []
+    adjoint_parts = []
+    grad_parts = []
+    leaving_all = []
+    for index in range(chunks):
+        part = slice(index * chunk_groups, (index + 1) * chunk_groups)
+        weights = (weight_one[:, part], bias_one[:, part], weight_two[:, part], bias_two[:, part])
+        arrived = arrivals[index]
+        if index > 0:
+            arrived, leaving_all[index - 1] = lax.optimization_barrier(
+                (arrived, leaving_all[index - 1])
+            )
+        leaving_rows, chunk_grads = chunk_spectral(arrived, tables, weights)
+        leaving_all.append(leaving_rows)
+        grad_parts.append(chunk_grads)
+    returns = [lax.all_to_all(rows, "lat", 0, 0, tiled=True) for rows in leaving_all]
+    for index in range(chunks):
+        returned = returns[index]
+        if index + 1 < chunks:
+            returned, _ = lax.optimization_barrier((returned, leaving_all[index + 1]))
+        filtered_parts.append(
+            jnp.einsum(
+                "jshmrc,wrjm->shwc", returned[:, :, :, :, :2], weighted_blocks, precision=HIGHEST
+            )
+        )
+        adjoint_parts.append(
+            jnp.einsum("jshmrc,wrjm->shwc", returned[:, :, :, :, 2:], lon_blocks, precision=HIGHEST)
+        )
+    local_grads = tuple(
+        jnp.concatenate([grads[slot] for grads in grad_parts], axis=1) for slot in range(4)
+    )
+    local_grads, _ = lax.optimization_barrier((local_grads, returns[-1]))
+    spectral_grads = flat_sum(local_grads, ("sample", "lat"))
+    filtered = jnp.concatenate(filtered_parts, axis=-1)
     block_out = (float_tokens + normed + filtered).astype(jnp.bfloat16)
-    normed_grad = upstream_out + jnp.einsum(
-        "jshrmc,wrjm->shwc", returned[:, :, :, 2:], lon_blocks, precision=HIGHEST
-    )
+    normed_grad = upstream_out + jnp.concatenate(adjoint_parts, axis=-1)
     hat_grad = normed_grad * norm_gain
     hat_mean = jnp.mean(hat_grad, axis=-1, keepdims=True)
     cross_mean = jnp.mean(hat_grad * normalized, axis=-1, keepdims=True)
     grad_input = upstream_out + inverse_std * (hat_grad - hat_mean - normalized * cross_mean)
     local_gain = jnp.sum(normed_grad * normalized, axis=(0, 1, 2))
     local_shift = jnp.sum(normed_grad, axis=(0, 1, 2))
-    summed = flat_sum(
-        (
-            weight_one_grad,
-            bias_one_grad,
-            weight_two_grad,
-            bias_two_grad,
-            local_gain,
-            local_shift,
-        ),
-        ("sample", "lat"),
-    )
+    norm_grads = flat_sum((local_gain, local_shift), ("sample", "lat"))
     return (
         block_out,
         grad_input.astype(jnp.bfloat16),
-        summed[4],
-        summed[5],
-        summed[0],
-        summed[1],
-        summed[2],
-        summed[3],
+        norm_grads[0],
+        norm_grads[1],
+        spectral_grads[0],
+        spectral_grads[1],
+        spectral_grads[2],
+        spectral_grads[3],
     )
 
 

time: 414 us -> 422 us (1.019)
  starting transfers between devices: 24.6 us -> 71.4 us
  blocking collectives: 45.3 us -> 0 us
  waiting for transfers between devices: 160 us -> 136 us
  other arithmetic: 18.4 us -> 28.3 us
  matrix products: 82.8 us -> 92.1 us
  local copies, waits for them, and re-layouts: 74.4 us -> 82.7 us
    all_to_all x1 -> x0, blocking collectives: 45.3 us -> none  [flat_sum(): reduced = lax.all_to_all(flat, axes, 0, 0, tiled=True).sum(axis=0)]
    all_to_all x2 -> x6, starting transfers between devices: 18.9 us -> 59.9 us  [the longest x2 20.2 us: local(): lax.all_to_all(rows, 'lat', 0, 0, tiled=True)]
    all_to_all x2 -> x6, waiting for transfers between devices: 129 us -> 94 us  [the longest x2 47.2 us: flat_sum(): reduced = lax.all_to_all(flat, axes, 0, 0, tiled=True).sum(axis=0)]
    all_to_all x1 -> x2, waiting for transfers between devices: 30.6 us -> 42.3 us  [flat_sum(): whole = lax.all_to_all(spread, axes, 0, 0, tiled=True).reshape(-1)]
    dot_general x8 -> x16, matrix products: 15.4 us -> 24.2 us  [product_part(): jnp.einsum('shkgi,gio->shkgo', part_in, weights[slot_index], precision=HI...]
    concatenate x2 -> x10, other arithmetic: 0.74 us -> 8.47 us  [the longest x4 3.68 us: local(): jnp.concatenate([grads[slot] for grads in grad_parts], axis=1)]
    slice x2 -> x4, local copies, waits for them, and re-layouts: 10.4 us -> 4.38 us  [the longest x1 3.69 us: local(): returned[:, :, :, :, 2:]]
    optimization_barrier x0 -> x3, local copies, waits for them, and re-layouts: none -> 5.86 us  [the longest x2 4.13 us: local(): lax.optimization_barrier((arrived, leaving_all[index - 1]))]
  transfers between devices with their start and end apart: 3 -> 8, of which waited for: 3 -> 6; matrix products, arithmetic and copies ran while one was open for 10% -> 35% of each run, Pallas kernels for 0% -> 0%
where the time goes in v3:
time: 422 us; the launch traced here: 414 us
  waiting for transfers between devices  136 us (32%)
  matrix products  92.1 us (22%)
  local copies, waits for them, and re-layouts  82.7 us (20%)
  starting transfers between devices  71.4 us (17%)
  other arithmetic  28.3 us (7%)
    all_to_all x2, waiting for transfers between devices, flat_sum(): reduced = lax.all_to_all(flat, axes, 0, 0, tiled=True).sum(axis=0)  47.2 us
    all_to_all x2, waiting for transfers between devices, flat_sum(): whole = lax.all_to_all(spread, axes, 0, 0, tiled=True).reshape(-1)  42.3 us
    all_to_all x2, waiting for transfers between devices, local(): arrivals.append(lax.all_to_all(leaving_modes, 'lat', 0, 0, tiled=True))  36.7 us
    dot_general x16, matrix products, product_part(): jnp.einsum('shkgi,gio->shkgo', part_in, weights[slot_index], precision=HI...  24.2 us
    all_to_all x2, starting transfers between devices, local(): lax.all_to_all(rows, 'lat', 0, 0, tiled=True)  20.2 us
    all_to_all x2, starting transfers between devices, flat_sum(): reduced = lax.all_to_all(flat, axes, 0, 0, tiled=True).sum(axis=0)  20.1 us
    dot_general x16, matrix products, contract(): jnp.einsum('shkgi,shkgo->gio', left_side, right_side, precision=HIGHEST)  20 us
    all_to_all x2, starting transfers between devices, local(): arrivals.append(lax.all_to_all(leaving_modes, 'lat', 0, 0, tiled=True))  19.7 us
  transfers between devices with their start and end apart: 8, of which 6 were waited for; matrix products, arithmetic and copies ran while one was open for 35% of the time, Pallas kernels for 0%

profile of v3, /device:TPU:1, one launch (start us, length us, event | category | flops | bytes accessed | tf_op | source)
XLA Modules:
  0.0 413.5 jit_solution(18245889791990940344)
XLA Ops:
  6.0 2.4 copy.253
  8.4 12.9 %all-to-all-start.1 = ((f32[32,1,3,3,4,384]{5,4,3,2,1,0:T(4,128)}), f32[32,1,3,3,4,384]{5,4,3,2,1,0:T(4,128)S(1)}, u32[]{:S(2)}, u32[]{:S(2)}) async-start(f32[32,1,3,3,4,384]{5,4,3,2,1,0:T(4,128)} %copy.253), calls=%async_computation.1 | async-start | bytes 3538944 | tf_op jit(solution)/shard_map/all_to_all | solution.py:193
  22.7 2.1 convolution_bitcast_fusion.17
  24.9 2.4 copy.252
  27.3 36.7 %all-to-all-done.1 = f32[32,1,3,3,4,384]{5,4,3,2,1,0:T(4,128)S(1)} async-done(((f32[32,1,3,3,4,384]{5,4,3,2,1,0:T(4,128)}), f32[32,1,3,3,4,384]{5,4,3,2,1,0:T(4,128)S(1)}, u32[]{:S(2)}, u32[]{:S(2)}) %all-to-all-start.1) | async-done | bytes 1769504 | tf_op jit(solution)/shard_map/all_to_all | solution.py:193
  64.0 6.8 %all-to-all-start = ((f32[32,1,3,3,4,384]{5,4,3,2,1,0:T(4,128)}), f32[32,1,3,3,4,384]{5,4,3,2,1,0:T(4,128)}, u32[]{:S(2)}, u32[]{:S(2)}) async-start(f32[32,1,3,3,4,384]{5,4,3,2,1,0:T(4,128)} %copy.252), calls=%async_computation | async-start | bytes 3538944 | tf_op jit(solution)/shard_map/all_to_all | solution.py:193
  71.6 2.1 convolution_bitcast_fusion.10
  73.7 2.1 convolution_bitcast_fusion.11
  86.1 1.5 fusion.70
  87.5 1.8 fusion.69
  90.3 2.2 stack.165
  92.5 2.2 stack.164
  94.7 2.0 copy_dynamic-update-slice_fusion.3
  96.6 1.7 convolution_add_fusion.6
  100.4 2.1 stack.162
  102.5 1.7 convolution_subtract_fusion.6
  106.2 2.2 stack.161
  110.7 2.6 fusion.376
  116.7 1.6 fusion.380
  120.8 2.1 stack.174
  124.3 1.6 copy.264
  134.2 1.7 copy.267
  135.9 2.1 convolution_bitcast_fusion.2
  139.2 2.1 convolution_bitcast_fusion.3
  144.0 3.2 fusion.113
  149.7 2.2 fusion.111
  155.6 1.5 fusion.76
  157.1 1.5 fusion.75
  158.6 2.4 copy.266
  161.0 10.0 %all-to-all-start.2 = ((f32[32,1,3,3,4,384]{5,4,3,2,1,0:T(4,128)}), f32[32,1,3,3,4,384]{5,4,3,2,1,0:T(4,128)}, u32[]{:S(2)}, u32[]{:S(2)}) async-start(f32[32,1,3,3,4,384]{5,4,3,2,1,0:T(4,128)} %copy.266), calls=%async_computation.2 | async-start | bytes 3538944 | tf_op jit(solution)/shard_map/all_to_all | solution.py:209
  171.1 2.4 slice_subtract_fusion
  173.5 2.2 stack.183
  175.7 2.2 stack.182
  179.2 1.8 convolution_add_fusion.2
  184.7 2.1 stack.180
  186.9 2.3 copy.272
  189.1 2.1 stack.179
  191.3 1.7 fusion.78
  195.6 1.6 fusion.382
  199.7 2.1 stack.192
  201.8 1.6 fusion.79
  203.4 1.6 fusion.16
  205.0 1.6 copy.277
  206.6 2.1 stack.191
  208.7 2.4 convolution_bitcast_fusion
  215.6 2.4 copy.280
  218.0 10.1 %all-to-all-start.3 = ((f32[32,1,3,3,4,384]{5,4,3,2,1,0:T(4,128)}), f32[32,1,3,3,4,384]{5,4,3,2,1,0:T(4,128)}, u32[]{:S(2)}, u32[]{:S(2)}) async-start(f32[32,1,3,3,4,384]{5,4,3,2,1,0:T(4,128)} %copy.280), calls=%async_computation.3 | async-start | bytes 3538944 | tf_op jit(solution)/shard_map/all_to_all | solution.py:209
  230.8 2.5 convolution_bitcast_fusion.30
  234.6 2.4 convolution_bitcast_fusion.26
  252.6 1.7 copy.279
  256.6 10.1 %all-to-all-done.3 = f32[32,1,3,3,4,384]{5,4,3,2,1,0:T(4,128)} async-done(((f32[32,1,3,3,4,384]{5,4,3,2,1,0:T(4,128)}), f32[32,1,3,3,4,384]{5,4,3,2,1,0:T(4,128)}, u32[]{:S(2)}, u32[]{:S(2)}) %all-to-all-start.3) | async-done | bytes 1769504 | tf_op jit(solution)/shard_map/all_to_all | solution.py:209
  269.4 3.7 fusion.384
  276.2 14.4 %all-to-all-start.4 = ((f32[256,1,128]{2,1,0:T(1,128)}), f32[256,1,128]{2,1,0:T(1,128)S(1)}, u32[]{:S(2)}, u32[]{:S(2)}) async-start(f32[256,1,128]{2,1,0:T(1,128)} %bitcast.266), calls=%async_computation.4 | async-start | bytes 262144 | tf_op jit(solution)/shard_map/all_to_all | solution.py:96
  290.6 2.4 select_maximum_fusion
  293.0 10.5 %all-to-all-done.4 = f32[256,1,128]{2,1,0:T(1,128)S(1)} async-done(((f32[256,1,128]{2,1,0:T(1,128)}), f32[256,1,128]{2,1,0:T(1,128)S(1)}, u32[]{:S(2)}, u32[]{:S(2)}) %all-to-all-start.4) | async-done | bytes 131104 | tf_op jit(solution)/shard_map/all_to_all | solution.py:96
  303.4 5.7 %all-to-all-start.6 = ((f32[256,1,1280]{2,1,0:T(1,128)}), f32[256,1,1280]{2,1,0:T(1,128)S(1)}, u32[]{:S(2)}, u32[]{:S(2)}) async-start(f32[256,1,1280]{2,1,0:T(1,128)} %bitcast.754), calls=%async_computation.6 | async-start | bytes 2621440 | tf_op jit(solution)/shard_map/all_to_all | solution.py:96
  309.1 36.7 %all-to-all-done.6 = f32[256,1,1280]{2,1,0:T(1,128)S(1)} async-done(((f32[256,1,1280]{2,1,0:T(1,128)}), f32[256,1,1280]{2,1,0:T(1,128)S(1)}, u32[]{:S(2)}, u32[]{:S(2)}) %all-to-all-start.6) | async-done | bytes 1310752 | tf_op jit(solution)/shard_map/all_to_all | solution.py:96
  346.6 5.7 %all-to-all-start.5 = ((f32[256,1,128]{2,1,0:T(1,128)}), f32[256,1,128]{2,1,0:T(1,128)S(1)}, u32[]{:S(2)}, u32[]{:S(2)}) async-start(f32[256,1,128]{2,1,0:T(1,128)} %broadcast_in_dim.14), calls=%async_computation.5 | async-start | bytes 262144 | tf_op jit(solution)/shard_map/all_to_all | solution.py:98
  353.2 12.1 %all-to-all-done.5 = f32[256,1,128]{2,1,0:T(1,128)S(1)} async-done(((f32[256,1,128]{2,1,0:T(1,128)}), f32[256,1,128]{2,1,0:T(1,128)S(1)}, u32[]{:S(2)}, u32[]{:S(2)}) %all-to-all-start.5) | async-done | bytes 131104 | tf_op jit(solution)/shard_map/all_to_all | solution.py:98
  365.2 1.7 broadcast_in_dim.15
  366.9 5.7 %all-to-all-start.7 = ((f32[256,1,1280]{2,1,0:T(1,128)}), f32[256,1,1280]{2,1,0:T(1,128)S(1)}, u32[]{:S(2)}, u32[]{:S(2)}) async-start(f32[256,1,1280]{2,1,0:T(1,128)} %broadcast_in_dim.15), calls=%async_computation.7 | async-start | bytes 2621440 | tf_op jit(solution)/shard_map/all_to_all | solution.py:98
  372.7 2.3 convolution_bitcast_fusion.23
  376.4 2.2 fusion.12
  379.2 30.2 %all-to-all-done.7 = f32[256,1,1280]{2,1,0:T(1,128)S(1)} async-done(((f32[256,1,1280]{2,1,0:T(1,128)}), f32[256,1,1280]{2,1,0:T(1,128)S(1)}, u32[]{:S(2)}, u32[]{:S(2)}) %all-to-all-start.7) | async-done | bytes 1310752 | tf_op jit(solution)/shard_map/all_to_all | solution.py:98
  (281 shorter events, 99.1 us)
Async XLA Ops:
  0.6 1.5 copy-start.6
  0.6 2.4 copy-start.68
  0.7 2.4 copy-start.76
  0.7 21.4 %copy-start.72 = (f32[32,3]{0,1:T(4,128)}, f32[32,3]{0,1:T(4,128)S(1)}, u32[]{:S(2)}) copy-start(f32[32,3]{0,1:T(4,128)S(1)} %fusion.294) | copy-start | bytes 1156
  3.1 19.5 %copy-start.52 = (f32[180,1,32,3]{0,2,3,1:T(8,128)}, f32[180,1,32,3]{0,2,3,1:T(8,128)S(1)}, u32[]{:S(2)}) copy-start(f32[180,1,32,3]{0,2,3,1:T(8,128)S(1)} %get-tuple-element.66) | copy-start | bytes 207364
  3.1 19.5 %copy-start.54 = (f32[180,1,32,3]{0,2,3,1:T(8,128)}, f32[180,1,32,3]{0,2,3,1:T(8,128)S(1)}, u32[]{:S(2)}) copy-start(f32[180,1,32,3]{0,2,3,1:T(8,128)S(1)} %get-tuple-element.67) | copy-start | bytes 207364
  3.5 1.8 copy-start.23
  8.4 12.9 %copy-start.78 = (f32[2,8,96]{2,1,0:T(8,128)S(1)}, f32[2,8,96]{2,1,0:T(8,128)}, u32[]{:S(2)}) copy-start(f32[2,8,96]{2,1,0:T(8,128)} %param.14) | copy-start | bytes 18436
  8.4 55.7 %all-to-all-start.1 = ((f32[32,1,3,3,4,384]{5,4,3,2,1,0:T(4,128)}), f32[32,1,3,3,4,384]{5,4,3,2,1,0:T(4,128)S(1)}, u32[]{:S(2)}, u32[]{:S(2)}) async-start(f32[32,1,3,3,4,384]{5,4,3,2,1,0:T(4,128)} %copy.253), calls=%async_computation.1 | async-start | bytes 3538944 | tf_op jit(solution)/shard_map/all_to_all | solution.py:193
  21.3 3.5 copy-start.66
  24.9 2.4 copy-start.79
  64.0 70.1 %all-to-all-start = ((f32[32,1,3,3,4,384]{5,4,3,2,1,0:T(4,128)}), f32[32,1,3,3,4,384]{5,4,3,2,1,0:T(4,128)}, u32[]{:S(2)}, u32[]{:S(2)}) async-start(f32[32,1,3,3,4,384]{5,4,3,2,1,0:T(4,128)} %copy.252), calls=%async_computation | async-start | bytes 3538944 | tf_op jit(solution)/shard_map/all_to_all | solution.py:193
  78.9 4.7 %copy-start.8 = (f32[96,3,4,96]{0,3,1,2:T(8,128)}, f32[96,3,4,96]{0,3,1,2:T(8,128)S(1)}, u32[]{:S(2)}) copy-start(f32[96,3,4,96]{0,3,1,2:T(8,128)S(1)} %copy.285) | copy-start | bytes 1327108
  78.9 1.3 copy-start.20
  80.2 2.2 copy-start.12
  83.6 1.6 copy-start.36
  84.7 1.3 copy-start.16
  86.0 16.4 %copy-start.2 = (f32[1,96,2,3,4,96]{5,1,3,4,2,0:T(8,128)}, f32[1,96,2,3,4,96]{5,1,3,4,2,0:T(8,128)S(1)}, u32[]{:S(2)}) copy-start(f32[1,96,2,3,4,96]{5,1,3,4,2,0:T(8,128)S(1)} %multiply_multiply_fusion.5) | copy-start | bytes 2654212
  86.0 3.3 copy-start.43
  86.1 3.3 copy-start.44
  104.2 4.2 %copy-start.50 = (f32[1,96,2,3,4,96]{5,1,3,4,2,0:T(8,128)S(1)}, f32[1,96,2,3,4,96]{5,1,3,4,2,0:T(8,128)}, u32[]{:S(2)}) copy-start(f32[1,96,2,3,4,96]{5,1,3,4,2,0:T(8,128)} %copy_dynamic-update-slice_fusion.3) | copy-start | bytes 2654212
  108.4 2.3 copy-start.28
  108.4 2.3 copy-start.31
  124.2 3.0 copy-start.40
  144.0 9.1 %copy-start.10 = (f32[96,3,4,96]{0,3,1,2:T(8,128)}, f32[96,3,4,96]{0,3,1,2:T(8,128)S(1)}, u32[]{:S(2)}) copy-start(f32[96,3,4,96]{0,3,1,2:T(8,128)S(1)} %copy.289) | copy-start | bytes 1327108
  144.0 3.3 copy-start.60
  149.7 3.4 copy-start.14
  149.7 2.3 copy-start.21
  149.7 2.3 copy-start.58
  153.1 1.6 copy-start.32
  155.6 25.4 %copy-start.4 = (f32[1,96,2,3,4,96]{5,1,3,4,2,0:T(8,128)}, f32[1,96,2,3,4,96]{5,1,3,4,2,0:T(8,128)S(1)}, u32[]{:S(2)}) copy-start(f32[1,96,2,3,4,96]{5,1,3,4,2,0:T(8,128)S(1)} %multiply_multiply_fusion.4) | copy-start | bytes 2654212
  155.6 3.0 copy-start.25
  161.0 56.9 %all-to-all-start.2 = ((f32[32,1,3,3,4,384]{5,4,3,2,1,0:T(4,128)}), f32[32,1,3,3,4,384]{5,4,3,2,1,0:T(4,128)}, u32[]{:S(2)}, u32[]{:S(2)}) async-start(f32[32,1,3,3,4,384]{5,4,3,2,1,0:T(4,128)} %copy.266), calls=%async_computation.2 | async-start | bytes 3538944 | tf_op jit(solution)/shard_map/all_to_all | solution.py:209
  179.2 1.8 copy-start.57
  182.1 1.4 copy-start.29
  183.5 10.8 %copy-start = (f32[1,96,2,3,4,96]{5,1,3,4,2,0:T(8,128)}, f32[1,96,2,3,4,96]{5,1,3,4,2,0:T(8,128)S(1)}, u32[]{:S(2)}) copy-start(f32[1,96,2,3,4,96]{5,1,3,4,2,0:T(8,128)S(1)} %get-tuple-element.31) | copy-start | bytes 2654212
  191.2 1.7 copy-start.19
  195.6 1.6 copy-start.22
  208.7 2.4 copy-start.41
  208.7 2.4 copy-start.42
  217.9 10.2 %copy-start.74 = (f32[2,4,96]{2,1,0:T(4,128)S(1)}, f32[2,4,96]{2,1,0:T(4,128)}, u32[]{:S(2)}) copy-start(f32[2,4,96]{2,1,0:T(4,128)} %get-tuple-element.28) | copy-start | bytes 9220
  217.9 11.6 %copy-start.75 = (f32[2,4,96]{2,1,0:T(4,128)S(1)}, f32[2,4,96]{2,1,0:T(4,128)}, u32[]{:S(2)}) copy-start(f32[2,4,96]{2,1,0:T(4,128)} %get-tuple-element.32) | copy-start | bytes 9220
  218.0 48.7 %all-to-all-start.3 = ((f32[32,1,3,3,4,384]{5,4,3,2,1,0:T(4,128)}), f32[32,1,3,3,4,384]{5,4,3,2,1,0:T(4,128)}, u32[]{:S(2)}, u32[]{:S(2)}) async-start(f32[32,1,3,3,4,384]{5,4,3,2,1,0:T(4,128)} %copy.280), calls=%async_computation.3 | async-start | bytes 3538944 | tf_op jit(solution)/shard_map/all_to_all | solution.py:209
  228.1 5.2 %copy-start.3 = (f32[1,96,2,3,4,96]{5,1,3,4,2,0:T(8,128)S(1)}, f32[1,96,2,3,4,96]{5,1,3,4,2,0:T(8,128)}, u32[]{:S(2)}) copy-start(f32[1,96,2,3,4,96]{5,1,3,4,2,0:T(8,128)} %copy-done.2) | copy-start | bytes 2654212
  230.8 3.8 copy-start.1
  233.3 3.7 copy-start.5
  245.0 2.0 copy-start.15
  247.0 1.8 copy-start.9
  252.5 3.0 copy-start.53
  252.5 3.0 copy-start.55
  256.5 17.6 %copy-start.45 = (f32[1,3,180,384]{3,2,1,0:T(8,128)}, f32[1,3,180,384]{3,2,1,0:T(8,128)S(1)}, u32[]{:S(2)}) copy-start(f32[1,3,180,384]{3,2,1,0:T(8,128)S(1)} %convolution_bitcast_fusion.21) | copy-start | bytes 2488324
  256.5 11.5 %copy-start.71 = (f32[2,8,96]{2,1,0:T(8,128)S(1)}, f32[2,8,96]{2,1,0:T(8,128)}, u32[]{:S(2)}) copy-start(f32[2,8,96]{2,1,0:T(8,128)} %pad_maximum_fusion.7) | copy-start | bytes 18436
  256.5 11.5 %copy-start.70 = (f32[2,8,96]{2,1,0:T(8,128)S(1)}, f32[2,8,96]{2,1,0:T(8,128)}, u32[]{:S(2)}) copy-start(f32[2,8,96]{2,1,0:T(8,128)} %pad_maximum_fusion.8) | copy-start | bytes 18436
  256.5 11.6 %copy-start.49 = (f32[2,8,96,96]{3,2,1,0:T(8,128)S(1)}, f32[2,8,96,96]{3,2,1,0:T(8,128)}, u32[]{:S(2)}) copy-start(f32[2,8,96,96]{3,2,1,0:T(8,128)} %maximum_maximum_fusion.1) | copy-start | bytes 1769476
  273.1 1.4 copy-start.24
  273.1 1.4 copy-start.69
  276.2 27.2 %all-to-all-start.4 = ((f32[256,1,128]{2,1,0:T(1,128)}), f32[256,1,128]{2,1,0:T(1,128)S(1)}, u32[]{:S(2)}, u32[]{:S(2)}) async-start(f32[256,1,128]{2,1,0:T(1,128)} %bitcast.266), calls=%async_computation.4 | async-start | bytes 262144 | tf_op jit(solution)/shard_map/all_to_all | solution.py:96
  303.4 42.4 %all-to-all-start.6 = ((f32[256,1,1280]{2,1,0:T(1,128)}), f32[256,1,1280]{2,1,0:T(1,128)S(1)}, u32[]{:S(2)}, u32[]{:S(2)}) async-start(f32[256,1,1280]{2,1,0:T(1,128)} %bitcast.754), calls=%async_computation.6 | async-start | bytes 2621440 | tf_op jit(solution)/shard_map/all_to_all | solution.py:96
  346.6 18.6 %all-to-all-start.5 = ((f32[256,1,128]{2,1,0:T(1,128)}), f32[256,1,128]{2,1,0:T(1,128)S(1)}, u32[]{:S(2)}, u32[]{:S(2)}) async-start(f32[256,1,128]{2,1,0:T(1,128)} %broadcast_in_dim.14), calls=%async_computation.5 | async-start | bytes 262144 | tf_op jit(solution)/shard_map/all_to_all | solution.py:98
  366.9 5.8 %copy-start.73 = (f32[32,3]{0,1:T(4,128)S(1)}, f32[32,3]{0,1:T(4,128)}, u32[]{:S(2)}) copy-start(f32[32,3]{0,1:T(4,128)} %copy-done.72) | copy-start | bytes 1156
  366.9 42.5 %all-to-all-start.7 = ((f32[256,1,1280]{2,1,0:T(1,128)}), f32[256,1,1280]{2,1,0:T(1,128)S(1)}, u32[]{:S(2)}, u32[]{:S(2)}) async-start(f32[256,1,1280]{2,1,0:T(1,128)} %broadcast_in_dim.15), calls=%async_computation.7 | async-start | bytes 2621440 | tf_op jit(solution)/shard_map/all_to_all | solution.py:98
  372.7 2.3 copy-start.61
  375.0 1.4 copy-start.48
  375.0 1.4 copy-start.77
  (25 other events, 28.0 us)
